TPU v7x, 256 devices: a whole 4x4x8 slice. The times are simulated.
256 devices in a mesh: run: 32 (over z, x_lo, core), entry: 8 (over x_hi, y).
Axes of the slice: x: 4 (x_hi: 2, x_lo: 2; x = x_hi * 2 + x_lo), y: 4, z: 8, core: 2. Of those that a mesh axis runs over, the one named last changes fastest.
Arguments:
- gradients: bfloat16 [16384, 65536], P('run', 'entry'), may hold values from -6 to 6
- probes: bfloat16 [65536, 512], P(('entry', 'run')), may hold values from -0.0234375 to 0.0234375
Outputs:
- projected: float32 [512, 65536], P('run', 'entry')
All inputs are finite; a program needn't handle non-finite values.
Results may differ from a plain program's by a relative error of at most 0.0026.
Values may be sent and summed in bfloat16 or wider, within the bound.
No kernel may reach another device: no remote copies, remote signals or barrier semaphores. Data moves between devices by JAX's collectives and lax.ppermute only.
A program may use at most 128 MiB of HBM per device.

v0:
```python
import functools

import jax
import jax.numpy as jnp
from jax import lax
from jax.sharding import PartitionSpec as P

HI = lax.Precision.HIGHEST
BLOCK = 128


def _swap(x, axis, size, bit):
    perm = [(i, i ^ (1 << bit)) for i in range(size)]
    return lax.ppermute(x, axis, perm)


def all_reduce_halving(x, axis, size, bits):
    shape = x.shape
    x = x.reshape(-1)
    idx = lax.axis_index(axis)
    for bit in bits:
        mine = (idx >> bit) & 1
        halves = x.reshape(2, -1)
        keep = lax.dynamic_index_in_dim(halves, mine, 0, keepdims=False)
        send = lax.dynamic_index_in_dim(halves, 1 - mine, 0, keepdims=False)
        x = keep + _swap(send, axis, size, bit)
    for bit in reversed(bits):
        mine = (idx >> bit) & 1
        other = _swap(x, axis, size, bit)
        lo = jnp.where(mine == 0, x, other)
        hi = jnp.where(mine == 0, other, x)
        x = jnp.concatenate([lo, hi])
    return x.reshape(shape)


def all_reduce_a2a(x, axis, size):
    shape = x.shape
    blocks = x.reshape(size, -1)
    mine = jnp.sum(lax.all_to_all(blocks, axis, 0, 0), axis=0)
    full = lax.all_to_all(jnp.broadcast_to(mine, blocks.shape), axis, 0, 0)
    return full.reshape(shape)


def inverse_factor(gram):
    n = gram.shape[0]
    nb = n // BLOCK
    eye = jnp.eye(BLOCK, dtype=gram.dtype)
    cols = []
    inv_diag = []
    for j in range(nb):
        s = j * BLOCK
        panel = gram[s:, s:s + BLOCK]
        if j > 0:
            left = jnp.concatenate([c[s - k * BLOCK:] for k, c in enumerate(cols)], axis=1)
            top = left[:BLOCK]
            panel = panel - jnp.dot(left, top.T, precision=HI)
        ljj = jnp.linalg.cholesky(panel[:BLOCK])
        ijj = lax.linalg.triangular_solve(ljj, eye, left_side=True, lower=True)
        if j < nb - 1:
            below = jnp.dot(panel[BLOCK:], ijj.T, precision=HI)
            cols.append(jnp.concatenate([ljj, below], axis=0))
        else:
            cols.append(ljj)
        inv_diag.append(ijj)

    def lblock(i, k):
        return cols[k][(i - k) * BLOCK:(i - k + 1) * BLOCK]

    inv = [[None] * nb for _ in range(nb)]
    for i in range(nb):
        inv[i][i] = inv_diag[i]
        for j in range(i - 1, -1, -1):
            acc = jnp.dot(lblock(i, j), inv[j][j], precision=HI)
            for k in range(j + 1, i):
                acc = acc + jnp.dot(lblock(i, k), inv[k][j], precision=HI)
            inv[i][j] = -jnp.dot(inv_diag[i], acc, precision=HI)
    zero = jnp.zeros((BLOCK, BLOCK), gram.dtype)
    rows = [jnp.concatenate([inv[i][j] if j <= i else zero for j in range(nb)], axis=1) for i in range(nb)]
    return jnp.concatenate(rows, axis=0)


def per_device(runs, entries, gradients, probes):
    run_bits = list(range(runs.bit_length() - 1))
    partial_sketch = jnp.dot(
        gradients,
        lax.all_gather(probes, "run", axis=0, tiled=True),
        preferred_element_type=jnp.float32,
    )
    sketch = all_reduce_a2a(partial_sketch, "entry", entries)
    local_gram = jnp.dot(
        sketch.T, sketch, precision=HI, preferred_element_type=jnp.float32
    )
    gram = all_reduce_halving(local_gram, "run", runs, run_bits)
    inv = inverse_factor(gram)
    basis = jnp.dot(sketch, inv.T, precision=HI).astype(jnp.bfloat16)
    return reduce_scatter_projection(basis, gradients, runs)


def reduce_scatter_projection(basis, gradients, runs):
    nz = runs // 4
    probes = basis.shape[1]
    rows = probes // runs
    idx = lax.axis_index("run")
    core = idx % 2
    xlo = (idx // 2) % 2
    z = idx // 4
    cols = basis.reshape(basis.shape[0], nz, 2, 2, rows)

    def project(c):
        b = lax.dynamic_index_in_dim(cols, c, 3, keepdims=False).reshape(basis.shape[0], -1)
        out = lax.dot_general(b, gradients, (((0,), (0,)), ((), ())), preferred_element_type=jnp.float32)
        return out.reshape(nz, 2, rows, gradients.shape[1])

    sent = project(1 - core)
    got = lax.ppermute(sent, "run", [(i, i ^ 1) for i in range(runs)])
    own = project(core)

    split = rows // 2

    def ring(x, r0, step_sign):
        perm = [(i, (i + 4 * step_sign) % runs) for i in range(runs)]

        def part(d):
            return own[d, x, r0:r0 + split] + got[d, x, r0:r0 + split]

        acc = None
        for s in range(nz - 1):
            d = (z - step_sign * (1 + s)) % nz
            acc = lax.ppermute(part(d) if acc is None else acc + part(d), "run", perm)
        return acc + part(z)

    lo = jnp.concatenate([ring(0, 0, 1), ring(0, split, 1)], axis=0)
    hi = jnp.concatenate([ring(1, 0, -1), ring(1, split, -1)], axis=0)
    keep = jnp.where(xlo == 0, lo, hi)
    send = jnp.where(xlo == 0, hi, lo)
    return keep + lax.ppermute(send, "run", [(i, i ^ 2) for i in range(runs)])


def solution(mesh):
    placed = (P("run", "entry"), P(("entry", "run"), None))
    body = functools.partial(per_device, mesh.shape["run"], mesh.shape["entry"])
    return jax.shard_map(
        body, mesh=mesh, in_specs=placed, out_specs=P("run", "entry"), check_vma=False
    )
```

profile of v0, /device:TPU:96, one launch (start us, length us, event | category | flops | bytes accessed | tf_op | source)
XLA Modules:
  0.0 457.7 jit_solution(14897207912172175861)
XLA Ops:
  7.3 74.0 %all-gather.2.cloned.1.call-done = bf16[8192,512]{1,0:T(8,128)(2,1)} async-done(((bf16[256,512]{1,0:T(8,128)(2,1)}), bf16[8192,512]{1,0:T(8,128)(2,1)}) %all-gather.2.cloned.1.call-update) | async-done | bytes 8388624 | tf_op jit(solution)/shard_map/all_gather | solution.py:86
  81.3 9.4 %fusion.103 = f32[512,512]{1,0:T(8,128)S(1)} fusion(bf16[512,8192]{1,0:T(8,128)(2,1)} %param.5, bf16[8192,512]{1,0:T(8,128)(2,1)} %all-gather.2.cloned.1.call-done), kind=kOutput, calls=%fused_computation.188 | convolution fusion | flops 4294967296 | bytes 17825792 | tf_op jit(solution)/shard_map/dot_general | solution.py:84
  92.0 24.1 %all_to_all.16 = f32[8,1,32768]{2,1,0:T(1,128)S(1)} all-to-all(f32[8,1,32768]{2,1,0:T(1,128)S(1)} %all_to_all.13), channel_id=1, replica_groups=mesh['run'=32,'entry'=8] {'entry'}, dimensions={0} | all-to-all | bytes 2097152 | tf_op jit(solution)/shard_map/all_to_all | solution.py:39
  121.9 15.0 %all-to-all-done.1 = f32[8,1,32768]{2,1,0:T(1,128)S(1)} async-done(((f32[8,1,32768]{2,1,0:T(1,128)}), f32[8,1,32768]{2,1,0:T(1,128)S(1)}, u32[]{:S(2)}, u32[]{:S(2)}) %all-to-all-start.1) | async-done | bytes 1048608 | tf_op jit(solution)/shard_map/all_to_all | solution.py:40
  146.9 7.9 %collective-permute-done.1 = f32[65536]{0:T(1024)S(1)} collective-permute-done((f32[65536]{0:T(1024)S(1)}, f32[65536]{0:T(1024)S(1)}, u32[]{:S(2)}, u32[]{:S(2)}) %collective-permute-start.1) | collective-permute-done | bytes 262176 | tf_op jit(solution)/shard_map/ppermute | solution.py:14
  161.5 5.0 %collective-permute-done.3 = f32[16384]{0:T(1024)S(1)} collective-permute-done((f32[16384]{0:T(1024)S(1)}, f32[16384]{0:T(1024)S(1)}, u32[]{:S(2)}, u32[]{:S(2)}) %collective-permute-start.3) | collective-permute-done | bytes 65568 | tf_op jit(solution)/shard_map/ppermute | solution.py:14
  168.7 5.8 %collective-permute-done.4 = f32[8192]{0:T(1024)S(1)} collective-permute-done((f32[8192]{0:T(1024)S(1)}, f32[8192]{0:T(1024)S(1)}, u32[]{:S(2)}, u32[]{:S(2)}) %collective-permute-start.4) | collective-permute-done | bytes 32800 | tf_op jit(solution)/shard_map/ppermute | solution.py:14
  176.5 6.1 %collective-permute-done.5 = f32[8192]{0:T(1024)S(1)} collective-permute-done((f32[8192]{0:T(1024)S(1)}, f32[8192]{0:T(1024)S(1)}, u32[]{:S(2)}, u32[]{:S(2)}) %collective-permute-start.5) | collective-permute-done | bytes 32800 | tf_op jit(solution)/shard_map/ppermute | solution.py:14
  182.8 5.4 %collective-permute-done.6 = f32[16384]{0:T(1024)S(1)} collective-permute-done((f32[16384]{0:T(1024)S(1)}, f32[16384]{0:T(1024)S(1)}, u32[]{:S(2)}, u32[]{:S(2)}) %collective-permute-start.6) | collective-permute-done | bytes 65568 | tf_op jit(solution)/shard_map/ppermute | solution.py:14
  193.4 6.4 %collective-permute-done.8 = f32[65536]{0:T(1024)S(1)} collective-permute-done((f32[65536]{0:T(1024)S(1)}, f32[65536]{0:T(1024)S(1)}, u32[]{:S(2)}, u32[]{:S(2)}) %collective-permute-start.8) | collective-permute-done | bytes 262176 | tf_op jit(solution)/shard_map/ppermute | solution.py:14
  202.8 11.7 %cholesky.74 = f32[128,128]{1,0:T(8,128)S(1)} custom-call(f32[128,128]{1,0:T(8,128)S(1)} %fusion.74), custom_call_target="Cholesky" | custom-call | tf_op jit(solution)/shard_map/jit(cholesky)/cholesky | solution.py:57
  215.8 9.8 %custom-call.8 = f32[1,128,128]{1,2,0:T(8,128)S(1)} custom-call(f32[1,128,128]{2,1,0:T(8,128)S(1)} %fusion.59), custom_call_target="InvertDiagBlocksLowerTriangular" | custom-call | tf_op jit(solution)/shard_map/triangular_solve/custom-call.0 | solution.py:58
  227.9 11.7 %cholesky.85 = f32[128,128]{1,0:T(8,128)S(1)} custom-call(f32[128,128]{1,0:T(8,128)S(1)} %fusion.72), custom_call_target="Cholesky" | custom-call | tf_op jit(solution)/shard_map/jit(cholesky)/cholesky | solution.py:57
  241.0 10.0 %custom-call.9 = f32[1,128,128]{1,2,0:T(8,128)S(1)} custom-call(f32[1,128,128]{2,1,0:T(8,128)S(1)} %fusion.60), custom_call_target="InvertDiagBlocksLowerTriangular" | custom-call | tf_op jit(solution)/shard_map/triangular_solve/custom-call.0 | solution.py:58
  252.7 11.7 %cholesky.96 = f32[128,128]{1,0:T(8,128)S(1)} custom-call(f32[128,128]{1,0:T(8,128)S(1)} %fusion.70), custom_call_target="Cholesky" | custom-call | tf_op jit(solution)/shard_map/jit(cholesky)/cholesky | solution.py:57
  265.7 9.8 %custom-call.10 = f32[1,128,128]{1,2,0:T(8,128)S(1)} custom-call(f32[1,128,128]{2,1,0:T(8,128)S(1)} %fusion.61), custom_call_target="InvertDiagBlocksLowerTriangular" | custom-call | tf_op jit(solution)/shard_map/triangular_solve/custom-call.0 | solution.py:58
  278.4 11.9 %cholesky.107 = f32[128,128]{1,0:T(8,128)S(1)} custom-call(f32[128,128]{1,0:T(8,128)S(1)} %fusion.68), custom_call_target="Cholesky" | custom-call | tf_op jit(solution)/shard_map/jit(cholesky)/cholesky | solution.py:57
  291.7 9.8 %custom-call.11 = f32[1,128,128]{1,2,0:T(8,128)S(1)} custom-call(f32[1,128,128]{2,1,0:T(8,128)S(1)} %fusion.62), custom_call_target="InvertDiagBlocksLowerTriangular" | custom-call | tf_op jit(solution)/shard_map/triangular_solve/custom-call.0 | solution.py:58
  305.5 9.0 %fusion = f32[8,2,16,8192]{3,2,1,0:T(8,128)} fusion(bf16[512,8192]{1,0:T(8,128)(2,1)} %param.5, bf16[512,8,2,2,16]{0,4,3,2,1:T(8,128)(2,1)S(1)} %bitcast.168, s32[]{:T(128)S(6)} %select_n.346), kind=kOutput, calls=%fused_computation | convolution fusion | flops 2147483648 | bytes 17039364 | tf_op jit(solution)/shard_map/dot_general | solution.py:111
  315.0 5.7 %fusion.2 = f32[8,2,16,8192]{3,2,1,0:T(8,128)S(1)} fusion(bf16[512,8192]{1,0:T(8,128)(2,1)} %param.5, bf16[512,8,2,2,16]{0,4,3,2,1:T(8,128)(2,1)S(1)} %bitcast.169, s32[]{:T(128)S(6)} %select_n.342), kind=kOutput, calls=%fused_computation.2 | convolution fusion | flops 2147483648 | bytes 17039364 | tf_op jit(solution)/shard_map/dot_general | solution.py:111
  320.8 7.6 %collective-permute-done.10 = f32[8,2,16,8192]{3,2,1,0:T(8,128)} collective-permute-done((f32[8,2,16,8192]{3,2,1,0:T(8,128)}, f32[8,2,16,8192]{3,2,1,0:T(8,128)}, u32[]{:S(2)}, u32[]{:S(2)}) %collective-permute-start.10) | collective-permute-done | bytes 8388640 | tf_op jit(solution)/shard_map/ppermute | solution.py:115
  333.9 5.1 %collective-permute-done.11 = f32[8,8192]{1,0:T(8,128)S(1)} collective-permute-done((f32[8,8192]{1,0:T(8,128)S(1)}, f32[8,8192]{1,0:T(8,128)S(1)}, u32[]{:S(2)}, u32[]{:S(2)}) %collective-permute-start.11) | collective-permute-done | bytes 262176 | tf_op jit(solution)/shard_map/ppermute | solution.py:129
  352.2 5.1 %collective-permute-done.12 = f32[8,8192]{1,0:T(8,128)S(1)} collective-permute-done((f32[8,8192]{1,0:T(8,128)S(1)}, f32[8,8192]{1,0:T(8,128)S(1)}, u32[]{:S(2)}, u32[]{:S(2)}) %collective-permute-start.12) | collective-permute-done | bytes 262176 | tf_op jit(solution)/shard_map/ppermute | solution.py:129
  440.6 9.2 %collective-permute-done.39 = f32[16,8192]{1,0:T(8,128)S(1)} collective-permute-done((f32[16,8192]{1,0:T(8,128)S(1)}, f32[16,8192]{1,0:T(8,128)S(1)}, u32[]{:S(2)}, u32[]{:S(2)}) %collective-permute-start.39) | collective-permute-done | bytes 524320 | tf_op jit(solution)/shard_map/ppermute | solution.py:136
  (177 shorter events, 156.0 us)
Async XLA Ops:
  6.5 74.8 %all-gather.2.cloned.1.call-start = ((), (), s32[]{:S(2)}) async-start(), calls=%async_computation.2 | async-start | bytes 8650752 | tf_op jit(solution)/shard_map/all_gather | solution.py:86
  118.4 18.6 %all-to-all-start.1 = ((f32[8,1,32768]{2,1,0:T(1,128)}), f32[8,1,32768]{2,1,0:T(1,128)S(1)}, u32[]{:S(2)}, u32[]{:S(2)}) async-start(f32[8,1,32768]{2,1,0:T(1,128)} %broadcast_in_dim.7), calls=%async_computation.1 | async-start | bytes 2097152 | tf_op jit(solution)/shard_map/all_to_all | solution.py:40
  314.5 13.9 %collective-permute-start.10 = (f32[8,2,16,8192]{3,2,1,0:T(8,128)}, f32[8,2,16,8192]{3,2,1,0:T(8,128)}, u32[]{:S(2)}, u32[]{:S(2)}) collective-permute-start(f32[8,2,16,8192]{3,2,1,0:T(8,128)} %fusion), channel_id=1, source_target_pairs={{0,8},{8,0},{16,24},{24,16},{32,40},{40,32},{48,56},{56,48},{64,72... | collective-permute-start | bytes 25165832 | tf_op jit(solution)/shard_map/ppermute | solution.py:115
  329.8 9.3 %collective-permute-start.11 = (f32[8,8192]{1,0:T(8,128)S(1)}, f32[8,8192]{1,0:T(8,128)S(1)}, u32[]{:S(2)}, u32[]{:S(2)}) collective-permute-start(f32[8,8192]{1,0:T(8,128)S(1)} %get-tuple-element.35), channel_id=1, source_target_pairs={{0,32},{8,40},{16,48},{24,56},{32,64},{40,72},{48,80},{56,88},{64,... | collective-permute-start | bytes 786440 | tf_op jit(solution)/shard_map/ppermute | solution.py:129
  331.5 12.3 %collective-permute-start.18 = (f32[8,8192]{1,0:T(8,128)S(1)}, f32[8,8192]{1,0:T(8,128)S(1)}, u32[]{:S(2)}, u32[]{:S(2)}) collective-permute-start(f32[8,8192]{1,0:T(8,128)S(1)} %get-tuple-element.38), channel_id=1, source_target_pairs={{0,32},{8,40},{16,48},{24,56},{32,64},{40,72},{48,80},{56,88},{64,... | collective-permute-start | bytes 786440 | tf_op jit(solution)/shard_map/ppermute | solution.py:129
  331.5 12.2 %collective-permute-start.25 = (f32[8,8192]{1,0:T(8,128)S(1)}, f32[8,8192]{1,0:T(8,128)S(1)}, u32[]{:S(2)}, u32[]{:S(2)}) collective-permute-start(f32[8,8192]{1,0:T(8,128)S(1)} %get-tuple-element.37), channel_id=1, source_target_pairs={{0,224},{8,232},{16,240},{24,248},{32,0},{40,8},{48,16},{56,24},{6... | collective-permute-start | bytes 786440 | tf_op jit(solution)/shard_map/ppermute | solution.py:129
  333.5 13.0 %collective-permute-start.32 = (f32[8,8192]{1,0:T(8,128)S(1)}, f32[8,8192]{1,0:T(8,128)S(1)}, u32[]{:S(2)}, u32[]{:S(2)}) collective-permute-start(f32[8,8192]{1,0:T(8,128)S(1)} %get-tuple-element.36), channel_id=1, source_target_pairs={{0,224},{8,232},{16,240},{24,248},{32,0},{40,8},{48,16},{56,24},{6... | collective-permute-start | bytes 786440 | tf_op jit(solution)/shard_map/ppermute | solution.py:129
  348.1 9.3 %collective-permute-start.12 = (f32[8,8192]{1,0:T(8,128)S(1)}, f32[8,8192]{1,0:T(8,128)S(1)}, u32[]{:S(2)}, u32[]{:S(2)}) collective-permute-start(f32[8,8192]{1,0:T(8,128)S(1)} %get-tuple-element.31), channel_id=1, source_target_pairs={{0,32},{8,40},{16,48},{24,56},{32,64},{40,72},{48,80},{56,88},{64,... | collective-permute-start | bytes 786440 | tf_op jit(solution)/shard_map/ppermute | solution.py:129
  348.4 12.6 %collective-permute-start.19 = (f32[8,8192]{1,0:T(8,128)S(1)}, f32[8,8192]{1,0:T(8,128)S(1)}, u32[]{:S(2)}, u32[]{:S(2)}) collective-permute-start(f32[8,8192]{1,0:T(8,128)S(1)} %get-tuple-element.34), channel_id=1, source_target_pairs={{0,32},{8,40},{16,48},{24,56},{32,64},{40,72},{48,80},{56,88},{64,... | collective-permute-start | bytes 786440 | tf_op jit(solution)/shard_map/ppermute | solution.py:129
  349.4 11.6 %collective-permute-start.26 = (f32[8,8192]{1,0:T(8,128)S(1)}, f32[8,8192]{1,0:T(8,128)S(1)}, u32[]{:S(2)}, u32[]{:S(2)}) collective-permute-start(f32[8,8192]{1,0:T(8,128)S(1)} %get-tuple-element.33), channel_id=1, source_target_pairs={{0,224},{8,232},{16,240},{24,248},{32,0},{40,8},{48,16},{56,24},{6... | collective-permute-start | bytes 786440 | tf_op jit(solution)/shard_map/ppermute | solution.py:129
  350.4 12.5 %collective-permute-start.33 = (f32[8,8192]{1,0:T(8,128)S(1)}, f32[8,8192]{1,0:T(8,128)S(1)}, u32[]{:S(2)}, u32[]{:S(2)}) collective-permute-start(f32[8,8192]{1,0:T(8,128)S(1)} %get-tuple-element.32), channel_id=1, source_target_pairs={{0,224},{8,232},{16,240},{24,248},{32,0},{40,8},{48,16},{56,24},{6... | collective-permute-start | bytes 786440 | tf_op jit(solution)/shard_map/ppermute | solution.py:129
  364.5 8.7 %collective-permute-start.13 = (f32[8,8192]{1,0:T(8,128)S(1)}, f32[8,8192]{1,0:T(8,128)S(1)}, u32[]{:S(2)}, u32[]{:S(2)}) collective-permute-start(f32[8,8192]{1,0:T(8,128)S(1)} %get-tuple-element.27), channel_id=1, source_target_pairs={{0,32},{8,40},{16,48},{24,56},{32,64},{40,72},{48,80},{56,88},{64,... | collective-permute-start | bytes 786440 | tf_op jit(solution)/shard_map/ppermute | solution.py:129
  364.9 11.1 %collective-permute-start.20 = (f32[8,8192]{1,0:T(8,128)S(1)}, f32[8,8192]{1,0:T(8,128)S(1)}, u32[]{:S(2)}, u32[]{:S(2)}) collective-permute-start(f32[8,8192]{1,0:T(8,128)S(1)} %get-tuple-element.30), channel_id=1, source_target_pairs={{0,32},{8,40},{16,48},{24,56},{32,64},{40,72},{48,80},{56,88},{64,... | collective-permute-start | bytes 786440 | tf_op jit(solution)/shard_map/ppermute | solution.py:129
  366.7 9.3 %collective-permute-start.27 = (f32[8,8192]{1,0:T(8,128)S(1)}, f32[8,8192]{1,0:T(8,128)S(1)}, u32[]{:S(2)}, u32[]{:S(2)}) collective-permute-start(f32[8,8192]{1,0:T(8,128)S(1)} %get-tuple-element.29), channel_id=1, source_target_pairs={{0,224},{8,232},{16,240},{24,248},{32,0},{40,8},{48,16},{56,24},{6... | collective-permute-start | bytes 786440 | tf_op jit(solution)/shard_map/ppermute | solution.py:129
  367.0 11.8 %collective-permute-start.34 = (f32[8,8192]{1,0:T(8,128)S(1)}, f32[8,8192]{1,0:T(8,128)S(1)}, u32[]{:S(2)}, u32[]{:S(2)}) collective-permute-start(f32[8,8192]{1,0:T(8,128)S(1)} %get-tuple-element.28), channel_id=1, source_target_pairs={{0,224},{8,232},{16,240},{24,248},{32,0},{40,8},{48,16},{56,24},{6... | collective-permute-start | bytes 786440 | tf_op jit(solution)/shard_map/ppermute | solution.py:129
  380.6 10.0 %collective-permute-start.21 = (f32[8,8192]{1,0:T(8,128)S(1)}, f32[8,8192]{1,0:T(8,128)S(1)}, u32[]{:S(2)}, u32[]{:S(2)}) collective-permute-start(f32[8,8192]{1,0:T(8,128)S(1)} %get-tuple-element.26), channel_id=1, source_target_pairs={{0,32},{8,40},{16,48},{24,56},{32,64},{40,72},{48,80},{56,88},{64,... | collective-permute-start | bytes 786440 | tf_op jit(solution)/shard_map/ppermute | solution.py:129
  381.7 9.0 %collective-permute-start.28 = (f32[8,8192]{1,0:T(8,128)S(1)}, f32[8,8192]{1,0:T(8,128)S(1)}, u32[]{:S(2)}, u32[]{:S(2)}) collective-permute-start(f32[8,8192]{1,0:T(8,128)S(1)} %get-tuple-element.25), channel_id=1, source_target_pairs={{0,224},{8,232},{16,240},{24,248},{32,0},{40,8},{48,16},{56,24},{6... | collective-permute-start | bytes 786440 | tf_op jit(solution)/shard_map/ppermute | solution.py:129
  382.7 9.3 %collective-permute-start.35 = (f32[8,8192]{1,0:T(8,128)S(1)}, f32[8,8192]{1,0:T(8,128)S(1)}, u32[]{:S(2)}, u32[]{:S(2)}) collective-permute-start(f32[8,8192]{1,0:T(8,128)S(1)} %get-tuple-element.24), channel_id=1, source_target_pairs={{0,224},{8,232},{16,240},{24,248},{32,0},{40,8},{48,16},{56,24},{6... | collective-permute-start | bytes 786440 | tf_op jit(solution)/shard_map/ppermute | solution.py:129
  396.9 10.6 %collective-permute-start.36 = (f32[8,8192]{1,0:T(8,128)S(1)}, f32[8,8192]{1,0:T(8,128)S(1)}, u32[]{:S(2)}, u32[]{:S(2)}) collective-permute-start(f32[8,8192]{1,0:T(8,128)S(1)} %get-tuple-element.20), channel_id=1, source_target_pairs={{0,224},{8,232},{16,240},{24,248},{32,0},{40,8},{48,16},{56,24},{6... | collective-permute-start | bytes 786440 | tf_op jit(solution)/shard_map/ppermute | solution.py:129
  409.2 10.8 %collective-permute-start.23 = (f32[8,8192]{1,0:T(8,128)S(1)}, f32[8,8192]{1,0:T(8,128)S(1)}, u32[]{:S(2)}, u32[]{:S(2)}) collective-permute-start(f32[8,8192]{1,0:T(8,128)S(1)} %get-tuple-element.18), channel_id=1, source_target_pairs={{0,32},{8,40},{16,48},{24,56},{32,64},{40,72},{48,80},{56,88},{64,... | collective-permute-start | bytes 786440 | tf_op jit(solution)/shard_map/ppermute | solution.py:129
  409.9 10.1 %collective-permute-start.30 = (f32[8,8192]{1,0:T(8,128)S(1)}, f32[8,8192]{1,0:T(8,128)S(1)}, u32[]{:S(2)}, u32[]{:S(2)}) collective-permute-start(f32[8,8192]{1,0:T(8,128)S(1)} %get-tuple-element.17), channel_id=1, source_target_pairs={{0,224},{8,232},{16,240},{24,248},{32,0},{40,8},{48,16},{56,24},{6... | collective-permute-start | bytes 786440 | tf_op jit(solution)/shard_map/ppermute | solution.py:129
  411.3 10.3 %collective-permute-start.37 = (f32[8,8192]{1,0:T(8,128)S(1)}, f32[8,8192]{1,0:T(8,128)S(1)}, u32[]{:S(2)}, u32[]{:S(2)}) collective-permute-start(f32[8,8192]{1,0:T(8,128)S(1)} %get-tuple-element.16), channel_id=1, source_target_pairs={{0,224},{8,232},{16,240},{24,248},{32,0},{40,8},{48,16},{56,24},{6... | collective-permute-start | bytes 786440 | tf_op jit(solution)/shard_map/ppermute | solution.py:129
  428.4 10.4 %collective-permute-start.38 = (f32[8,8192]{1,0:T(8,128)S(1)}, f32[8,8192]{1,0:T(8,128)S(1)}, u32[]{:S(2)}, u32[]{:S(2)}) collective-permute-start(f32[8,8192]{1,0:T(8,128)S(1)} %get-tuple-element.12), channel_id=1, source_target_pairs={{0,224},{8,232},{16,240},{24,248},{32,0},{40,8},{48,16},{56,24},{6... | collective-permute-start | bytes 786440 | tf_op jit(solution)/shard_map/ppermute | solution.py:129
  440.5 9.3 %collective-permute-start.39 = (f32[16,8192]{1,0:T(8,128)S(1)}, f32[16,8192]{1,0:T(8,128)S(1)}, u32[]{:S(2)}, u32[]{:S(2)}) collective-permute-start(f32[16,8192]{1,0:T(8,128)S(1)} %fusion.29), channel_id=1, source_target_pairs={{0,16},{8,24},{16,0},{24,8},{32,48},{40,56},{48,32},{56,40},{64,80... | collective-permute-start | bytes 1572872 | tf_op jit(solution)/shard_map/ppermute | solution.py:136
  (19 other events, 121.6 us)
Sparse Core Ops, SparseCore 0:
  9.2 72.0 all-gather.1
where the time goes:
time: 467 us; the launch traced here: 458 us
  waiting for transfers between devices  225 us (48%)
  other arithmetic  109 us (23%)
  starting transfers between devices  41.9 us (9%)
  matrix products  35.7 us (8%)
  blocking collectives  24.1 us (5%)
  between operations  14.4 us (3%)
  local copies, waits for them, and re-layouts  7.45 us (2%)
    all_gather x1, waiting for transfers between devices, per_device(): lax.all_gather(probes, 'run', axis=0, tiled=True)  74 us
    ppermute x28, waiting for transfers between devices, ring(): acc = lax.ppermute(part(d) if acc is None else acc + part(d), 'run', perm)  69.1 us
    another operation x12, other arithmetic, inverse_factor(): ljj = jnp.linalg.cholesky(panel[:BLOCK])  49.7 us
    ppermute x10, waiting for transfers between devices, _swap(): return lax.ppermute(x, axis, perm)  49.2 us
    another operation x8, other arithmetic, inverse_factor(): ijj = lax.linalg.triangular_solve(ljj, eye, left_side=True, lower=True)  42 us
    ppermute x28, starting transfers between devices, ring(): acc = lax.ppermute(part(d) if acc is None else acc + part(d), 'run', perm)  30 us
    all_to_all x1, blocking collectives, all_reduce_a2a(): mine = jnp.sum(lax.all_to_all(blocks, axis, 0, 0), axis=0)  24.1 us
    all_to_all x1, waiting for transfers between devices, all_reduce_a2a(): full = lax.all_to_all(jnp.broadcast_to(mine, blocks.shape), axis, 0, 0)  15 us
  transfers between devices with their start and end apart: 42, of which 37 were waited for; matrix products, arithmetic and copies ran while one was open for 1% of the time, Pallas kernels for 0%

commit v1 on v0

--- a/solution.py
+++ b/solution.py
@@ -6,6 +6,8 @@
 from jax.sharding import PartitionSpec as P
 
 HI = lax.Precision.HIGHEST
+RUN = ("z", "xlo", "core")
+ENTRY = ("xhi", "y")
 BLOCK = 128
 
 
@@ -79,18 +81,47 @@
     return jnp.concatenate(rows, axis=0)
 
 
+def gathered_sketch(gradients, probes, runs):
+    nz = runs // 4
+    z = lax.axis_index("z")
+    xlo = lax.axis_index("xlo")
+    core = lax.axis_index("core")
+    pair = [(0, 1), (1, 0)]
+    other = lax.ppermute(probes, "xlo", pair)
+    by_xlo = jnp.stack([jnp.where(xlo == 0, probes, other), jnp.where(xlo == 0, other, probes)])
+    other = lax.ppermute(by_xlo, "core", pair)
+    chip = jnp.stack([jnp.where(core == 0, by_xlo, other), jnp.where(core == 0, other, by_xlo)], axis=1)
+    chip = chip.reshape(2, 2 * probes.shape[0], probes.shape[1])
+    half = lax.dynamic_index_in_dim(chip, core, 0, keepdims=False)
+
+    def hops(step, count):
+        perm = [(r, ((r // 4 + step) % nz) * 4 + r % 4) for r in range(runs)]
+        out, cur = [], half
+        for _ in range(count):
+            cur = lax.ppermute(cur, RUN, perm)
+            out.append(cur)
+        return out
+
+    ahead, behind = hops(1, nz // 2), hops(-1, (nz - 1) // 2)
+    mine = [half] + ahead + behind
+    where_from = [z] + [(z - k) % nz for k in range(1, len(ahead) + 1)] + [(z + k) % nz for k in range(1, len(behind) + 1)]
+    theirs = lax.ppermute(jnp.stack(mine), "core", pair)
+    full = jnp.zeros((nz,) + chip.shape, chip.dtype)
+    zero = jnp.zeros((), z.dtype)
+    for j, zi in enumerate(where_from):
+        full = lax.dynamic_update_slice(full, mine[j][None, None], (zi, core, zero, zero))
+        full = lax.dynamic_update_slice(full, theirs[j][None, None], (zi, 1 - core, zero, zero))
+    return jnp.dot(gradients, full.reshape(-1, probes.shape[1]), preferred_element_type=jnp.float32)
+
+
 def per_device(runs, entries, gradients, probes):
     run_bits = list(range(runs.bit_length() - 1))
-    partial_sketch = jnp.dot(
-        gradients,
-        lax.all_gather(probes, "run", axis=0, tiled=True),
-        preferred_element_type=jnp.float32,
-    )
-    sketch = all_reduce_a2a(partial_sketch, "entry", entries)
+    partial_sketch = gathered_sketch(gradients, probes, runs)
+    sketch = all_reduce_a2a(partial_sketch, ENTRY, entries)
     local_gram = jnp.dot(
         sketch.T, sketch, precision=HI, preferred_element_type=jnp.float32
     )
-    gram = all_reduce_halving(local_gram, "run", runs, run_bits)
+    gram = all_reduce_halving(local_gram, RUN, runs, run_bits)
     inv = inverse_factor(gram)
     basis = jnp.dot(sketch, inv.T, precision=HI).astype(jnp.bfloat16)
     return reduce_scatter_projection(basis, gradients, runs)
@@ -100,7 +131,7 @@
     nz = runs // 4
     probes = basis.shape[1]
     rows = probes // runs
-    idx = lax.axis_index("run")
+    idx = lax.axis_index(RUN)
     core = idx % 2
     xlo = (idx // 2) % 2
     z = idx // 4
@@ -112,7 +143,7 @@
         return out.reshape(nz, 2, rows, gradients.shape[1])
 
     sent = project(1 - core)
-    got = lax.ppermute(sent, "run", [(i, i ^ 1) for i in range(runs)])
+    got = lax.ppermute(sent, RUN, [(i, i ^ 1) for i in range(runs)])
     own = project(core)
 
     split = rows // 2
@@ -126,19 +157,21 @@
         acc = None
         for s in range(nz - 1):
             d = (z - step_sign * (1 + s)) % nz
-            acc = lax.ppermute(part(d) if acc is None else acc + part(d), "run", perm)
+            acc = lax.ppermute(part(d) if acc is None else acc + part(d), RUN, perm)
         return acc + part(z)
 
     lo = jnp.concatenate([ring(0, 0, 1), ring(0, split, 1)], axis=0)
     hi = jnp.concatenate([ring(1, 0, -1), ring(1, split, -1)], axis=0)
     keep = jnp.where(xlo == 0, lo, hi)
     send = jnp.where(xlo == 0, hi, lo)
-    return keep + lax.ppermute(send, "run", [(i, i ^ 2) for i in range(runs)])
+    return keep + lax.ppermute(send, RUN, [(i, i ^ 2) for i in range(runs)])
 
 
 def solution(mesh):
-    placed = (P("run", "entry"), P(("entry", "run"), None))
-    body = functools.partial(per_device, mesh.shape["run"], mesh.shape["entry"])
+    runs, entries = mesh.shape["run"], mesh.shape["entry"]
+    split = jax.sharding.Mesh(mesh.devices.reshape(runs // 4, 2, 2, 2, entries // 2), RUN + ENTRY)
+    placed = (P(RUN, ENTRY), P(ENTRY + RUN, None))
+    body = functools.partial(per_device, runs, entries)
     return jax.shard_map(
-        body, mesh=mesh, in_specs=placed, out_specs=P("run", "entry"), check_vma=False
+        body, mesh=split, in_specs=placed, out_specs=P(RUN, ENTRY), check_vma=False
     )

time: 467 us -> 460 us (0.985)
  the two profiles are of different devices: /device:TPU:96 before, /device:TPU:8 now
where the time goes in v1:
time: 460 us; the launch traced here: 454 us
  waiting for transfers between devices  195 us (42%)
  other arithmetic  111 us (24%)
  starting transfers between devices  68 us (15%)
  matrix products  30.8 us (7%)
  local copies, waits for them, and re-layouts  25 us (5%)
  blocking collectives  22.8 us (5%)
    ppermute x28, waiting for transfers between devices, ring(): acc = lax.ppermute(part(d) if acc is None else acc + part(d), RUN, perm)  57.9 us
    another operation x12, other arithmetic, inverse_factor(): ljj = jnp.linalg.cholesky(panel[:BLOCK])  49.7 us
    ppermute x10, waiting for transfers between devices, _swap(): return lax.ppermute(x, axis, perm)  45.7 us
    ppermute x7, waiting for transfers between devices, hops(): cur = lax.ppermute(cur, RUN, perm)  45.2 us
    another operation x8, other arithmetic, inverse_factor(): ijj = lax.linalg.triangular_solve(ljj, eye, left_side=True, lower=True)  42.2 us
    ppermute x28, starting transfers between devices, ring(): acc = lax.ppermute(part(d) if acc is None else acc + part(d), RUN, perm)  37.6 us
    all_to_all x1, blocking collectives, all_reduce_a2a(): mine = jnp.sum(lax.all_to_all(blocks, axis, 0, 0), axis=0)  22.8 us
    dot_general x2, matrix products, project(): lax.dot_general(b, gradients, (((0,), (0,)), ((), ())), preferred_element...  14.8 us
  transfers between devices with their start and end apart: 51, of which 42 were waited for; matrix products, arithmetic and copies ran while one was open for 3% of the time, Pallas kernels for 0%

profile of v1, /device:TPU:8, one launch (start us, length us, event | category | flops | bytes accessed | tf_op | source)
XLA Modules:
  0.0 454.0 jit_solution(13914073624911145174)
XLA Ops:
  1.5 6.8 %collective-permute-done = bf16[256,512]{1,0:T(8,128)(2,1)S(1)} collective-permute-done((bf16[256,512]{1,0:T(8,128)(2,1)}, bf16[256,512]{1,0:T(8,128)(2,1)S(1)}, u32[]{:S(2)}, u32[]{:S(2)}) %collective-permute-start) | collective-permute-done | bytes 262176 | tf_op jit(solution)/shard_map/ppermute | solution.py:90
  14.3 16.2 %collective-permute-done.2 = bf16[512,512]{1,0:T(8,128)(2,1)S(1)} collective-permute-done((bf16[512,512]{1,0:T(8,128)(2,1)S(1)}, bf16[512,512]{1,0:T(8,128)(2,1)S(1)}, u32[]{:S(2)}, u32[]{:S(2)}) %collective-permute-start.2) | collective-permute-done | bytes 524320 | tf_op jit(solution)/shard_map/ppermute | solution.py:101
  33.7 11.4 %collective-permute-done.3 = bf16[512,512]{1,0:T(8,128)(2,1)S(1)} collective-permute-done((bf16[512,512]{1,0:T(8,128)(2,1)S(1)}, bf16[512,512]{1,0:T(8,128)(2,1)S(1)}, u32[]{:S(2)}, u32[]{:S(2)}) %collective-permute-start.3) | collective-permute-done | bytes 524320 | tf_op jit(solution)/shard_map/ppermute | solution.py:101
  48.3 10.5 %collective-permute-done.4 = bf16[512,512]{1,0:T(8,128)(2,1)S(1)} collective-permute-done((bf16[512,512]{1,0:T(8,128)(2,1)S(1)}, bf16[512,512]{1,0:T(8,128)(2,1)S(1)}, u32[]{:S(2)}, u32[]{:S(2)}) %collective-permute-start.4) | collective-permute-done | bytes 524320 | tf_op jit(solution)/shard_map/ppermute | solution.py:101
  64.6 7.1 %collective-permute-done.5 = bf16[512,512]{1,0:T(8,128)(2,1)S(1)} collective-permute-done((bf16[512,512]{1,0:T(8,128)(2,1)S(1)}, bf16[512,512]{1,0:T(8,128)(2,1)S(1)}, u32[]{:S(2)}, u32[]{:S(2)}) %collective-permute-start.5) | collective-permute-done | bytes 524320 | tf_op jit(solution)/shard_map/ppermute | solution.py:101
  76.6 6.4 %collective-permute-done.9 = bf16[8,512,512]{2,1,0:T(8,128)(2,1)} collective-permute-done((bf16[8,512,512]{2,1,0:T(8,128)(2,1)}, bf16[8,512,512]{2,1,0:T(8,128)(2,1)}, u32[]{:S(2)}, u32[]{:S(2)}) %collective-permute-start.9) | collective-permute-done | bytes 4194336 | tf_op jit(solution)/shard_map/ppermute | solution.py:108
  98.5 22.8 %all_to_all.16 = f32[8,1,32768]{2,1,0:T(1,128)S(1)} all-to-all(f32[8,1,32768]{2,1,0:T(1,128)S(1)} %all_to_all.13), channel_id=1, replica_groups=mesh['z'=8,'xlo'=2,'core'=2,'xhi'=2,'y'=4] {'xhi','y'}, dimensions={0} | all-to-all | bytes 2097152 | tf_op jit(solution)/shard_map/all_to_all | solution.py:41
  123.7 5.7 %all-to-all-start.1 = ((f32[8,1,32768]{2,1,0:T(1,128)}), f32[8,1,32768]{2,1,0:T(1,128)S(1)}, u32[]{:S(2)}, u32[]{:S(2)}) async-start(f32[8,1,32768]{2,1,0:T(1,128)} %broadcast_in_dim.43), calls=%async_computation.1 | async-start | bytes 2097152 | tf_op jit(solution)/shard_map/all_to_all | solution.py:42
  129.4 13.4 %all-to-all-done.1 = f32[8,1,32768]{2,1,0:T(1,128)S(1)} async-done(((f32[8,1,32768]{2,1,0:T(1,128)}), f32[8,1,32768]{2,1,0:T(1,128)S(1)}, u32[]{:S(2)}, u32[]{:S(2)}) %all-to-all-start.1) | async-done | bytes 1048608 | tf_op jit(solution)/shard_map/all_to_all | solution.py:42
  152.7 7.8 %collective-permute-done.11 = f32[65536]{0:T(1024)S(1)} collective-permute-done((f32[65536]{0:T(1024)S(1)}, f32[65536]{0:T(1024)S(1)}, u32[]{:S(2)}, u32[]{:S(2)}) %collective-permute-start.11) | collective-permute-done | bytes 262176 | tf_op jit(solution)/shard_map/ppermute | solution.py:16
  188.2 5.3 %collective-permute-done.16 = f32[16384]{0:T(1024)S(1)} collective-permute-done((f32[16384]{0:T(1024)S(1)}, f32[16384]{0:T(1024)S(1)}, u32[]{:S(2)}, u32[]{:S(2)}) %collective-permute-start.16) | collective-permute-done | bytes 65568 | tf_op jit(solution)/shard_map/ppermute | solution.py:16
  199.2 5.8 %collective-permute-done.18 = f32[65536]{0:T(1024)S(1)} collective-permute-done((f32[65536]{0:T(1024)S(1)}, f32[65536]{0:T(1024)S(1)}, u32[]{:S(2)}, u32[]{:S(2)}) %collective-permute-start.18) | collective-permute-done | bytes 262176 | tf_op jit(solution)/shard_map/ppermute | solution.py:16
  207.6 11.7 %cholesky.74 = f32[128,128]{1,0:T(8,128)S(1)} custom-call(f32[128,128]{1,0:T(8,128)S(1)} %fusion.82), custom_call_target="Cholesky" | custom-call | tf_op jit(solution)/shard_map/jit(cholesky)/cholesky | solution.py:59
  220.7 9.8 %custom-call.8 = f32[1,128,128]{1,2,0:T(8,128)S(1)} custom-call(f32[1,128,128]{2,1,0:T(8,128)S(1)} %fusion.67), custom_call_target="InvertDiagBlocksLowerTriangular" | custom-call | tf_op jit(solution)/shard_map/triangular_solve/custom-call.0 | solution.py:60
  231.9 11.7 %cholesky.85 = f32[128,128]{1,0:T(8,128)S(1)} custom-call(f32[128,128]{1,0:T(8,128)S(1)} %fusion.80), custom_call_target="Cholesky" | custom-call | tf_op jit(solution)/shard_map/jit(cholesky)/cholesky | solution.py:59
  245.0 10.2 %custom-call.9 = f32[1,128,128]{1,2,0:T(8,128)S(1)} custom-call(f32[1,128,128]{2,1,0:T(8,128)S(1)} %fusion.68), custom_call_target="InvertDiagBlocksLowerTriangular" | custom-call | tf_op jit(solution)/shard_map/triangular_solve/custom-call.0 | solution.py:60
  257.8 11.7 %cholesky.96 = f32[128,128]{1,0:T(8,128)S(1)} custom-call(f32[128,128]{1,0:T(8,128)S(1)} %fusion.78), custom_call_target="Cholesky" | custom-call | tf_op jit(solution)/shard_map/jit(cholesky)/cholesky | solution.py:59
  270.8 9.8 %custom-call.10 = f32[1,128,128]{1,2,0:T(8,128)S(1)} custom-call(f32[1,128,128]{2,1,0:T(8,128)S(1)} %fusion.69), custom_call_target="InvertDiagBlocksLowerTriangular" | custom-call | tf_op jit(solution)/shard_map/triangular_solve/custom-call.0 | solution.py:60
  282.3 11.9 %cholesky.107 = f32[128,128]{1,0:T(8,128)S(1)} custom-call(f32[128,128]{1,0:T(8,128)S(1)} %fusion.76), custom_call_target="Cholesky" | custom-call | tf_op jit(solution)/shard_map/jit(cholesky)/cholesky | solution.py:59
  295.5 9.8 %custom-call.11 = f32[1,128,128]{1,2,0:T(8,128)S(1)} custom-call(f32[1,128,128]{2,1,0:T(8,128)S(1)} %fusion.70), custom_call_target="InvertDiagBlocksLowerTriangular" | custom-call | tf_op jit(solution)/shard_map/triangular_solve/custom-call.0 | solution.py:60
  310.5 9.0 %fusion = f32[8,2,16,8192]{3,2,1,0:T(8,128)} fusion(bf16[512,8192]{1,0:T(8,128)(2,1)} %param.5, bf16[512,8,2,2,16]{0,4,3,2,1:T(8,128)(2,1)S(1)} %bitcast.251, s32[]{:T(128)S(6)} %select_n.475), kind=kOutput, calls=%fused_computation | convolution fusion | flops 2147483648 | bytes 17039364 | tf_op jit(solution)/shard_map/dot_general | solution.py:142
  319.9 5.7 %fusion.2 = f32[8,2,16,8192]{3,2,1,0:T(8,128)S(1)} fusion(bf16[512,8192]{1,0:T(8,128)(2,1)} %param.5, bf16[512,8,2,2,16]{0,4,3,2,1:T(8,128)(2,1)S(1)} %bitcast.252, s32[]{:T(128)S(6)} %select_n.471), kind=kOutput, calls=%fused_computation.2 | convolution fusion | flops 2147483648 | bytes 17039364 | tf_op jit(solution)/shard_map/dot_general | solution.py:142
  325.6 7.6 %collective-permute-done.20 = f32[8,2,16,8192]{3,2,1,0:T(8,128)} collective-permute-done((f32[8,2,16,8192]{3,2,1,0:T(8,128)}, f32[8,2,16,8192]{3,2,1,0:T(8,128)}, u32[]{:S(2)}, u32[]{:S(2)}) %collective-permute-start.20) | collective-permute-done | bytes 8388640 | tf_op jit(solution)/shard_map/ppermute | solution.py:146
  442.5 10.1 %collective-permute-done.49 = f32[16,8192]{1,0:T(8,128)S(1)} collective-permute-done((f32[16,8192]{1,0:T(8,128)S(1)}, f32[16,8192]{1,0:T(8,128)S(1)}, u32[]{:S(2)}, u32[]{:S(2)}) %collective-permute-start.49) | collective-permute-done | bytes 524320 | tf_op jit(solution)/shard_map/ppermute | solution.py:167
  (245 shorter events, 214.1 us)
Async XLA Ops:
  12.4 18.1 %collective-permute-start.2 = (bf16[512,512]{1,0:T(8,128)(2,1)S(1)}, bf16[512,512]{1,0:T(8,128)(2,1)S(1)}, u32[]{:S(2)}, u32[]{:S(2)}) collective-permute-start(bf16[512,512]{1,0:T(8,128)(2,1)S(1)} %get-tuple-element.43), channel_id=1, source_target_pairs={{0,32},{8,40},{16,48},{24,56},{32,64},{40,72},{48,80},{56,88},{64,... | collective-permute-start | bytes 1572872 | tf_op jit(solution)/shard_map/ppermute | solution.py:101
  30.5 14.6 %collective-permute-start.3 = (bf16[512,512]{1,0:T(8,128)(2,1)S(1)}, bf16[512,512]{1,0:T(8,128)(2,1)S(1)}, u32[]{:S(2)}, u32[]{:S(2)}) collective-permute-start(bf16[512,512]{1,0:T(8,128)(2,1)S(1)} %collective-permute-done.2), channel_id=1, source_target_pairs={{0,32},{8,40},{16,48},{24,56},{32,64},{40,72},{48,80},{56,88},{64,... | collective-permute-start | bytes 1572872 | tf_op jit(solution)/shard_map/ppermute | solution.py:101
  30.5 14.6 %collective-permute-start.6 = (bf16[512,512]{1,0:T(8,128)(2,1)S(1)}, bf16[512,512]{1,0:T(8,128)(2,1)S(1)}, u32[]{:S(2)}, u32[]{:S(2)}) collective-permute-start(bf16[512,512]{1,0:T(8,128)(2,1)S(1)} %get-tuple-element.43), channel_id=1, source_target_pairs={{0,224},{8,232},{16,240},{24,248},{32,0},{40,8},{48,16},{56,24},{6... | collective-permute-start | bytes 1572872 | tf_op jit(solution)/shard_map/ppermute | solution.py:101
  45.1 13.7 %collective-permute-start.4 = (bf16[512,512]{1,0:T(8,128)(2,1)S(1)}, bf16[512,512]{1,0:T(8,128)(2,1)S(1)}, u32[]{:S(2)}, u32[]{:S(2)}) collective-permute-start(bf16[512,512]{1,0:T(8,128)(2,1)S(1)} %collective-permute-done.3), channel_id=1, source_target_pairs={{0,32},{8,40},{16,48},{24,56},{32,64},{40,72},{48,80},{56,88},{64,... | collective-permute-start | bytes 1572872 | tf_op jit(solution)/shard_map/ppermute | solution.py:101
  45.1 14.6 %collective-permute-start.7 = (bf16[512,512]{1,0:T(8,128)(2,1)S(1)}, bf16[512,512]{1,0:T(8,128)(2,1)S(1)}, u32[]{:S(2)}, u32[]{:S(2)}) collective-permute-start(bf16[512,512]{1,0:T(8,128)(2,1)S(1)} %collective-permute-done.6), channel_id=1, source_target_pairs={{0,224},{8,232},{16,240},{24,248},{32,0},{40,8},{48,16},{56,24},{6... | collective-permute-start | bytes 1572872 | tf_op jit(solution)/shard_map/ppermute | solution.py:101
  58.8 12.9 %collective-permute-start.5 = (bf16[512,512]{1,0:T(8,128)(2,1)S(1)}, bf16[512,512]{1,0:T(8,128)(2,1)S(1)}, u32[]{:S(2)}, u32[]{:S(2)}) collective-permute-start(bf16[512,512]{1,0:T(8,128)(2,1)S(1)} %collective-permute-done.4), channel_id=1, source_target_pairs={{0,32},{8,40},{16,48},{24,56},{32,64},{40,72},{48,80},{56,88},{64,... | collective-permute-start | bytes 1572872 | tf_op jit(solution)/shard_map/ppermute | solution.py:101
  59.7 14.6 %collective-permute-start.8 = (bf16[512,512]{1,0:T(8,128)(2,1)S(1)}, bf16[512,512]{1,0:T(8,128)(2,1)S(1)}, u32[]{:S(2)}, u32[]{:S(2)}) collective-permute-start(bf16[512,512]{1,0:T(8,128)(2,1)S(1)} %collective-permute-done.7), channel_id=1, source_target_pairs={{0,224},{8,232},{16,240},{24,248},{32,0},{40,8},{48,16},{56,24},{6... | collective-permute-start | bytes 1572872 | tf_op jit(solution)/shard_map/ppermute | solution.py:101
  123.7 19.2 %all-to-all-start.1 = ((f32[8,1,32768]{2,1,0:T(1,128)}), f32[8,1,32768]{2,1,0:T(1,128)S(1)}, u32[]{:S(2)}, u32[]{:S(2)}) async-start(f32[8,1,32768]{2,1,0:T(1,128)} %broadcast_in_dim.43), calls=%async_computation.1 | async-start | bytes 2097152 | tf_op jit(solution)/shard_map/all_to_all | solution.py:42
  319.6 13.7 %collective-permute-start.20 = (f32[8,2,16,8192]{3,2,1,0:T(8,128)}, f32[8,2,16,8192]{3,2,1,0:T(8,128)}, u32[]{:S(2)}, u32[]{:S(2)}) collective-permute-start(f32[8,2,16,8192]{3,2,1,0:T(8,128)} %fusion), channel_id=1, source_target_pairs={{0,8},{8,0},{16,24},{24,16},{32,40},{40,32},{48,56},{56,48},{64,72... | collective-permute-start | bytes 25165832 | tf_op jit(solution)/shard_map/ppermute | solution.py:146
  334.6 10.5 %collective-permute-start.21 = (f32[8,8192]{1,0:T(8,128)S(1)}, f32[8,8192]{1,0:T(8,128)S(1)}, u32[]{:S(2)}, u32[]{:S(2)}) collective-permute-start(f32[8,8192]{1,0:T(8,128)S(1)} %get-tuple-element.35), channel_id=1, source_target_pairs={{0,32},{8,40},{16,48},{24,56},{32,64},{40,72},{48,80},{56,88},{64,... | collective-permute-start | bytes 786440 | tf_op jit(solution)/shard_map/ppermute | solution.py:160
  334.8 10.3 %collective-permute-start.42 = (f32[8,8192]{1,0:T(8,128)S(1)}, f32[8,8192]{1,0:T(8,128)S(1)}, u32[]{:S(2)}, u32[]{:S(2)}) collective-permute-start(f32[8,8192]{1,0:T(8,128)S(1)} %get-tuple-element.36), channel_id=1, source_target_pairs={{0,224},{8,232},{16,240},{24,248},{32,0},{40,8},{48,16},{56,24},{6... | collective-permute-start | bytes 786440 | tf_op jit(solution)/shard_map/ppermute | solution.py:160
  337.9 11.2 %collective-permute-start.35 = (f32[8,8192]{1,0:T(8,128)S(1)}, f32[8,8192]{1,0:T(8,128)S(1)}, u32[]{:S(2)}, u32[]{:S(2)}) collective-permute-start(f32[8,8192]{1,0:T(8,128)S(1)} %get-tuple-element.37), channel_id=1, source_target_pairs={{0,224},{8,232},{16,240},{24,248},{32,0},{40,8},{48,16},{56,24},{6... | collective-permute-start | bytes 786440 | tf_op jit(solution)/shard_map/ppermute | solution.py:160
  338.7 11.1 %collective-permute-start.28 = (f32[8,8192]{1,0:T(8,128)S(1)}, f32[8,8192]{1,0:T(8,128)S(1)}, u32[]{:S(2)}, u32[]{:S(2)}) collective-permute-start(f32[8,8192]{1,0:T(8,128)S(1)} %get-tuple-element.38), channel_id=1, source_target_pairs={{0,32},{8,40},{16,48},{24,56},{32,64},{40,72},{48,80},{56,88},{64,... | collective-permute-start | bytes 786440 | tf_op jit(solution)/shard_map/ppermute | solution.py:160
  351.5 10.5 %collective-permute-start.22 = (f32[8,8192]{1,0:T(8,128)S(1)}, f32[8,8192]{1,0:T(8,128)S(1)}, u32[]{:S(2)}, u32[]{:S(2)}) collective-permute-start(f32[8,8192]{1,0:T(8,128)S(1)} %get-tuple-element.31), channel_id=1, source_target_pairs={{0,32},{8,40},{16,48},{24,56},{32,64},{40,72},{48,80},{56,88},{64,... | collective-permute-start | bytes 786440 | tf_op jit(solution)/shard_map/ppermute | solution.py:160
  351.6 10.4 %collective-permute-start.43 = (f32[8,8192]{1,0:T(8,128)S(1)}, f32[8,8192]{1,0:T(8,128)S(1)}, u32[]{:S(2)}, u32[]{:S(2)}) collective-permute-start(f32[8,8192]{1,0:T(8,128)S(1)} %get-tuple-element.32), channel_id=1, source_target_pairs={{0,224},{8,232},{16,240},{24,248},{32,0},{40,8},{48,16},{56,24},{6... | collective-permute-start | bytes 786440 | tf_op jit(solution)/shard_map/ppermute | solution.py:160
  354.8 10.3 %collective-permute-start.36 = (f32[8,8192]{1,0:T(8,128)S(1)}, f32[8,8192]{1,0:T(8,128)S(1)}, u32[]{:S(2)}, u32[]{:S(2)}) collective-permute-start(f32[8,8192]{1,0:T(8,128)S(1)} %get-tuple-element.33), channel_id=1, source_target_pairs={{0,224},{8,232},{16,240},{24,248},{32,0},{40,8},{48,16},{56,24},{6... | collective-permute-start | bytes 786440 | tf_op jit(solution)/shard_map/ppermute | solution.py:160
  367.6 9.7 %collective-permute-start.23 = (f32[8,8192]{1,0:T(8,128)S(1)}, f32[8,8192]{1,0:T(8,128)S(1)}, u32[]{:S(2)}, u32[]{:S(2)}) collective-permute-start(f32[8,8192]{1,0:T(8,128)S(1)} %get-tuple-element.27), channel_id=1, source_target_pairs={{0,32},{8,40},{16,48},{24,56},{32,64},{40,72},{48,80},{56,88},{64,... | collective-permute-start | bytes 786440 | tf_op jit(solution)/shard_map/ppermute | solution.py:160
  370.9 9.7 %collective-permute-start.37 = (f32[8,8192]{1,0:T(8,128)S(1)}, f32[8,8192]{1,0:T(8,128)S(1)}, u32[]{:S(2)}, u32[]{:S(2)}) collective-permute-start(f32[8,8192]{1,0:T(8,128)S(1)} %get-tuple-element.29), channel_id=1, source_target_pairs={{0,224},{8,232},{16,240},{24,248},{32,0},{40,8},{48,16},{56,24},{6... | collective-permute-start | bytes 786440 | tf_op jit(solution)/shard_map/ppermute | solution.py:160
  382.8 10.3 %collective-permute-start.24 = (f32[8,8192]{1,0:T(8,128)S(1)}, f32[8,8192]{1,0:T(8,128)S(1)}, u32[]{:S(2)}, u32[]{:S(2)}) collective-permute-start(f32[8,8192]{1,0:T(8,128)S(1)} %get-tuple-element.23), channel_id=1, source_target_pairs={{0,32},{8,40},{16,48},{24,56},{32,64},{40,72},{48,80},{56,88},{64,... | collective-permute-start | bytes 786440 | tf_op jit(solution)/shard_map/ppermute | solution.py:160
  398.0 10.2 %collective-permute-start.25 = (f32[8,8192]{1,0:T(8,128)S(1)}, f32[8,8192]{1,0:T(8,128)S(1)}, u32[]{:S(2)}, u32[]{:S(2)}) collective-permute-start(f32[8,8192]{1,0:T(8,128)S(1)} %get-tuple-element.19), channel_id=1, source_target_pairs={{0,32},{8,40},{16,48},{24,56},{32,64},{40,72},{48,80},{56,88},{64,... | collective-permute-start | bytes 786440 | tf_op jit(solution)/shard_map/ppermute | solution.py:160
  412.9 9.9 %collective-permute-start.26 = (f32[8,8192]{1,0:T(8,128)S(1)}, f32[8,8192]{1,0:T(8,128)S(1)}, u32[]{:S(2)}, u32[]{:S(2)}) collective-permute-start(f32[8,8192]{1,0:T(8,128)S(1)} %get-tuple-element.15), channel_id=1, source_target_pairs={{0,32},{8,40},{16,48},{24,56},{32,64},{40,72},{48,80},{56,88},{64,... | collective-permute-start | bytes 786440 | tf_op jit(solution)/shard_map/ppermute | solution.py:160
  427.2 10.1 %collective-permute-start.27 = (f32[8,8192]{1,0:T(8,128)S(1)}, f32[8,8192]{1,0:T(8,128)S(1)}, u32[]{:S(2)}, u32[]{:S(2)}) collective-permute-start(f32[8,8192]{1,0:T(8,128)S(1)} %get-tuple-element.11), channel_id=1, source_target_pairs={{0,32},{8,40},{16,48},{24,56},{32,64},{40,72},{48,80},{56,88},{64,... | collective-permute-start | bytes 786440 | tf_op jit(solution)/shard_map/ppermute | solution.py:160
  427.5 9.8 %collective-permute-start.48 = (f32[8,8192]{1,0:T(8,128)S(1)}, f32[8,8192]{1,0:T(8,128)S(1)}, u32[]{:S(2)}, u32[]{:S(2)}) collective-permute-start(f32[8,8192]{1,0:T(8,128)S(1)} %get-tuple-element.12), channel_id=1, source_target_pairs={{0,224},{8,232},{16,240},{24,248},{32,0},{40,8},{48,16},{56,24},{6... | collective-permute-start | bytes 786440 | tf_op jit(solution)/shard_map/ppermute | solution.py:160
  441.8 10.8 %collective-permute-start.49 = (f32[16,8192]{1,0:T(8,128)S(1)}, f32[16,8192]{1,0:T(8,128)S(1)}, u32[]{:S(2)}, u32[]{:S(2)}) collective-permute-start(f32[16,8192]{1,0:T(8,128)S(1)} %fusion.37), channel_id=1, source_target_pairs={{0,16},{8,24},{16,0},{24,8},{32,48},{40,56},{48,32},{56,40},{64,80... | collective-permute-start | bytes 1572872 | tf_op jit(solution)/shard_map/ppermute | solution.py:167
  (38 other events, 320.6 us)

commit v2 on v1

--- a/solution.py
+++ b/solution.py
@@ -56,7 +56,7 @@
             left = jnp.concatenate([c[s - k * BLOCK:] for k, c in enumerate(cols)], axis=1)
             top = left[:BLOCK]
             panel = panel - jnp.dot(left, top.T, precision=HI)
-        ljj = jnp.linalg.cholesky(panel[:BLOCK])
+        ljj = lax.linalg.cholesky(panel[:BLOCK], symmetrize_input=False)
         ijj = lax.linalg.triangular_solve(ljj, eye, left_side=True, lower=True)
         if j < nb - 1:
             below = jnp.dot(panel[BLOCK:], ijj.T, precision=HI)

time: 460 us -> 460 us (level)
  no operation moved by 1% of the time
where the time goes in v2:
time: 460 us; the launch traced here: 454 us
  waiting for transfers between devices  195 us (42%)
  other arithmetic  111 us (24%)
  starting transfers between devices  68 us (15%)
  matrix products  31.2 us (7%)
  local copies, waits for them, and re-layouts  24.3 us (5%)
  blocking collectives  22.8 us (5%)
    ppermute x28, waiting for transfers between devices, ring(): acc = lax.ppermute(part(d) if acc is None else acc + part(d), RUN, perm)  57.9 us
    another operation x12, other arithmetic, inverse_factor(): ljj = lax.linalg.cholesky(panel[:BLOCK], symmetrize_input=False)  49.7 us
    ppermute x10, waiting for transfers between devices, _swap(): return lax.ppermute(x, axis, perm)  45.7 us
    ppermute x7, waiting for transfers between devices, hops(): cur = lax.ppermute(cur, RUN, perm)  45.2 us
    another operation x8, other arithmetic, inverse_factor(): ijj = lax.linalg.triangular_solve(ljj, eye, left_side=True, lower=True)  42.2 us
    ppermute x28, starting transfers between devices, ring(): acc = lax.ppermute(part(d) if acc is None else acc + part(d), RUN, perm)  37.6 us
    all_to_all x1, blocking collectives, all_reduce_a2a(): mine = jnp.sum(lax.all_to_all(blocks, axis, 0, 0), axis=0)  22.8 us
    dot_general x2, matrix products, project(): lax.dot_general(b, gradients, (((0,), (0,)), ((), ())), preferred_element...  14.8 us
  transfers between devices with their start and end apart: 51, of which 42 were waited for; matrix products, arithmetic and copies ran while one was open for 3% of the time, Pallas kernels for 0%

profile of v2, /device:TPU:8, one launch (start us, length us, event | category | flops | bytes accessed | tf_op | source)
XLA Modules:
  0.0 453.6 jit_solution(12401833445207726401)
XLA Ops:
  1.5 6.8 %collective-permute-done = bf16[256,512]{1,0:T(8,128)(2,1)S(1)} collective-permute-done((bf16[256,512]{1,0:T(8,128)(2,1)}, bf16[256,512]{1,0:T(8,128)(2,1)S(1)}, u32[]{:S(2)}, u32[]{:S(2)}) %collective-permute-start) | collective-permute-done | bytes 262176 | tf_op jit(solution)/shard_map/ppermute | solution.py:90
  14.3 16.2 %collective-permute-done.2 = bf16[512,512]{1,0:T(8,128)(2,1)S(1)} collective-permute-done((bf16[512,512]{1,0:T(8,128)(2,1)S(1)}, bf16[512,512]{1,0:T(8,128)(2,1)S(1)}, u32[]{:S(2)}, u32[]{:S(2)}) %collective-permute-start.2) | collective-permute-done | bytes 524320 | tf_op jit(solution)/shard_map/ppermute | solution.py:101
  33.7 11.4 %collective-permute-done.3 = bf16[512,512]{1,0:T(8,128)(2,1)S(1)} collective-permute-done((bf16[512,512]{1,0:T(8,128)(2,1)S(1)}, bf16[512,512]{1,0:T(8,128)(2,1)S(1)}, u32[]{:S(2)}, u32[]{:S(2)}) %collective-permute-start.3) | collective-permute-done | bytes 524320 | tf_op jit(solution)/shard_map/ppermute | solution.py:101
  48.3 10.5 %collective-permute-done.4 = bf16[512,512]{1,0:T(8,128)(2,1)S(1)} collective-permute-done((bf16[512,512]{1,0:T(8,128)(2,1)S(1)}, bf16[512,512]{1,0:T(8,128)(2,1)S(1)}, u32[]{:S(2)}, u32[]{:S(2)}) %collective-permute-start.4) | collective-permute-done | bytes 524320 | tf_op jit(solution)/shard_map/ppermute | solution.py:101
  64.6 7.1 %collective-permute-done.5 = bf16[512,512]{1,0:T(8,128)(2,1)S(1)} collective-permute-done((bf16[512,512]{1,0:T(8,128)(2,1)S(1)}, bf16[512,512]{1,0:T(8,128)(2,1)S(1)}, u32[]{:S(2)}, u32[]{:S(2)}) %collective-permute-start.5) | collective-permute-done | bytes 524320 | tf_op jit(solution)/shard_map/ppermute | solution.py:101
  76.6 6.4 %collective-permute-done.9 = bf16[8,512,512]{2,1,0:T(8,128)(2,1)} collective-permute-done((bf16[8,512,512]{2,1,0:T(8,128)(2,1)}, bf16[8,512,512]{2,1,0:T(8,128)(2,1)}, u32[]{:S(2)}, u32[]{:S(2)}) %collective-permute-start.9) | collective-permute-done | bytes 4194336 | tf_op jit(solution)/shard_map/ppermute | solution.py:108
  98.5 22.8 %all_to_all.16 = f32[8,1,32768]{2,1,0:T(1,128)S(1)} all-to-all(f32[8,1,32768]{2,1,0:T(1,128)S(1)} %all_to_all.13), channel_id=1, replica_groups=mesh['z'=8,'xlo'=2,'core'=2,'xhi'=2,'y'=4] {'xhi','y'}, dimensions={0} | all-to-all | bytes 2097152 | tf_op jit(solution)/shard_map/all_to_all | solution.py:41
  123.7 5.7 %all-to-all-start.1 = ((f32[8,1,32768]{2,1,0:T(1,128)}), f32[8,1,32768]{2,1,0:T(1,128)S(1)}, u32[]{:S(2)}, u32[]{:S(2)}) async-start(f32[8,1,32768]{2,1,0:T(1,128)} %broadcast_in_dim.39), calls=%async_computation.1 | async-start | bytes 2097152 | tf_op jit(solution)/shard_map/all_to_all | solution.py:42
  129.4 13.4 %all-to-all-done.1 = f32[8,1,32768]{2,1,0:T(1,128)S(1)} async-done(((f32[8,1,32768]{2,1,0:T(1,128)}), f32[8,1,32768]{2,1,0:T(1,128)S(1)}, u32[]{:S(2)}, u32[]{:S(2)}) %all-to-all-start.1) | async-done | bytes 1048608 | tf_op jit(solution)/shard_map/all_to_all | solution.py:42
  152.7 7.8 %collective-permute-done.11 = f32[65536]{0:T(1024)S(1)} collective-permute-done((f32[65536]{0:T(1024)S(1)}, f32[65536]{0:T(1024)S(1)}, u32[]{:S(2)}, u32[]{:S(2)}) %collective-permute-start.11) | collective-permute-done | bytes 262176 | tf_op jit(solution)/shard_map/ppermute | solution.py:16
  188.2 5.3 %collective-permute-done.16 = f32[16384]{0:T(1024)S(1)} collective-permute-done((f32[16384]{0:T(1024)S(1)}, f32[16384]{0:T(1024)S(1)}, u32[]{:S(2)}, u32[]{:S(2)}) %collective-permute-start.16) | collective-permute-done | bytes 65568 | tf_op jit(solution)/shard_map/ppermute | solution.py:16
  199.2 5.8 %collective-permute-done.18 = f32[65536]{0:T(1024)S(1)} collective-permute-done((f32[65536]{0:T(1024)S(1)}, f32[65536]{0:T(1024)S(1)}, u32[]{:S(2)}, u32[]{:S(2)}) %collective-permute-start.18) | collective-permute-done | bytes 262176 | tf_op jit(solution)/shard_map/ppermute | solution.py:16
  207.3 11.7 %custom-call.12 = f32[128,128]{1,0:T(8,128)S(1)} custom-call(f32[128,128]{1,0:T(8,128)S(1)} %slice.119), custom_call_target="Cholesky" | custom-call | tf_op jit(solution)/shard_map/cholesky/custom-call.1 | solution.py:59
  220.4 9.8 %custom-call.13 = f32[1,128,128]{1,2,0:T(8,128)S(1)} custom-call(f32[1,128,128]{2,1,0:T(8,128)S(1)} %fusion.67), custom_call_target="InvertDiagBlocksLowerTriangular" | custom-call | tf_op jit(solution)/shard_map/triangular_solve/custom-call.0 | solution.py:60
  231.6 11.7 %custom-call.14 = f32[128,128]{1,0:T(8,128)S(1)} custom-call(f32[128,128]{1,0:T(8,128)S(1)} %slice.123), custom_call_target="Cholesky" | custom-call | tf_op jit(solution)/shard_map/cholesky/custom-call.1 | solution.py:59
  244.6 10.2 %custom-call.15 = f32[1,128,128]{1,2,0:T(8,128)S(1)} custom-call(f32[1,128,128]{2,1,0:T(8,128)S(1)} %fusion.68), custom_call_target="InvertDiagBlocksLowerTriangular" | custom-call | tf_op jit(solution)/shard_map/triangular_solve/custom-call.0 | solution.py:60
  257.5 11.7 %custom-call.16 = f32[128,128]{1,0:T(8,128)S(1)} custom-call(f32[128,128]{1,0:T(8,128)S(1)} %slice.127), custom_call_target="Cholesky" | custom-call | tf_op jit(solution)/shard_map/cholesky/custom-call.1 | solution.py:59
  270.5 9.8 %custom-call.17 = f32[1,128,128]{1,2,0:T(8,128)S(1)} custom-call(f32[1,128,128]{2,1,0:T(8,128)S(1)} %fusion.69), custom_call_target="InvertDiagBlocksLowerTriangular" | custom-call | tf_op jit(solution)/shard_map/triangular_solve/custom-call.0 | solution.py:60
  281.9 11.9 %custom-call.18 = f32[128,128]{1,0:T(8,128)S(1)} custom-call(f32[128,128]{1,0:T(8,128)S(1)} %slice_subtract_fusion.2), custom_call_target="Cholesky" | custom-call | tf_op jit(solution)/shard_map/cholesky/custom-call.1 | solution.py:59
  295.1 9.8 %custom-call.19 = f32[1,128,128]{1,2,0:T(8,128)S(1)} custom-call(f32[1,128,128]{2,1,0:T(8,128)S(1)} %fusion.70), custom_call_target="InvertDiagBlocksLowerTriangular" | custom-call | tf_op jit(solution)/shard_map/triangular_solve/custom-call.0 | solution.py:60
  310.1 9.0 %fusion = f32[8,2,16,8192]{3,2,1,0:T(8,128)} fusion(bf16[512,8192]{1,0:T(8,128)(2,1)} %param.5, bf16[512,8,2,2,16]{0,4,3,2,1:T(8,128)(2,1)S(1)} %bitcast.235, s32[]{:T(128)S(6)} %select_n.488), kind=kOutput, calls=%fused_computation | convolution fusion | flops 2147483648 | bytes 17039364 | tf_op jit(solution)/shard_map/dot_general | solution.py:142
  319.5 5.7 %fusion.2 = f32[8,2,16,8192]{3,2,1,0:T(8,128)S(1)} fusion(bf16[512,8192]{1,0:T(8,128)(2,1)} %param.5, bf16[512,8,2,2,16]{0,4,3,2,1:T(8,128)(2,1)S(1)} %bitcast.236, s32[]{:T(128)S(6)} %select_n.484), kind=kOutput, calls=%fused_computation.2 | convolution fusion | flops 2147483648 | bytes 17039364 | tf_op jit(solution)/shard_map/dot_general | solution.py:142
  325.2 7.6 %collective-permute-done.20 = f32[8,2,16,8192]{3,2,1,0:T(8,128)} collective-permute-done((f32[8,2,16,8192]{3,2,1,0:T(8,128)}, f32[8,2,16,8192]{3,2,1,0:T(8,128)}, u32[]{:S(2)}, u32[]{:S(2)}) %collective-permute-start.20) | collective-permute-done | bytes 8388640 | tf_op jit(solution)/shard_map/ppermute | solution.py:146
  442.1 10.1 %collective-permute-done.49 = f32[16,8192]{1,0:T(8,128)S(1)} collective-permute-done((f32[16,8192]{1,0:T(8,128)S(1)}, f32[16,8192]{1,0:T(8,128)S(1)}, u32[]{:S(2)}, u32[]{:S(2)}) %collective-permute-start.49) | collective-permute-done | bytes 524320 | tf_op jit(solution)/shard_map/ppermute | solution.py:167
  (237 shorter events, 213.8 us)
Async XLA Ops:
  12.4 18.1 %collective-permute-start.2 = (bf16[512,512]{1,0:T(8,128)(2,1)S(1)}, bf16[512,512]{1,0:T(8,128)(2,1)S(1)}, u32[]{:S(2)}, u32[]{:S(2)}) collective-permute-start(bf16[512,512]{1,0:T(8,128)(2,1)S(1)} %get-tuple-element.43), channel_id=1, source_target_pairs={{0,32},{8,40},{16,48},{24,56},{32,64},{40,72},{48,80},{56,88},{64,... | collective-permute-start | bytes 1572872 | tf_op jit(solution)/shard_map/ppermute | solution.py:101
  30.5 14.6 %collective-permute-start.3 = (bf16[512,512]{1,0:T(8,128)(2,1)S(1)}, bf16[512,512]{1,0:T(8,128)(2,1)S(1)}, u32[]{:S(2)}, u32[]{:S(2)}) collective-permute-start(bf16[512,512]{1,0:T(8,128)(2,1)S(1)} %collective-permute-done.2), channel_id=1, source_target_pairs={{0,32},{8,40},{16,48},{24,56},{32,64},{40,72},{48,80},{56,88},{64,... | collective-permute-start | bytes 1572872 | tf_op jit(solution)/shard_map/ppermute | solution.py:101
  30.5 14.6 %collective-permute-start.6 = (bf16[512,512]{1,0:T(8,128)(2,1)S(1)}, bf16[512,512]{1,0:T(8,128)(2,1)S(1)}, u32[]{:S(2)}, u32[]{:S(2)}) collective-permute-start(bf16[512,512]{1,0:T(8,128)(2,1)S(1)} %get-tuple-element.43), channel_id=1, source_target_pairs={{0,224},{8,232},{16,240},{24,248},{32,0},{40,8},{48,16},{56,24},{6... | collective-permute-start | bytes 1572872 | tf_op jit(solution)/shard_map/ppermute | solution.py:101
  45.1 13.7 %collective-permute-start.4 = (bf16[512,512]{1,0:T(8,128)(2,1)S(1)}, bf16[512,512]{1,0:T(8,128)(2,1)S(1)}, u32[]{:S(2)}, u32[]{:S(2)}) collective-permute-start(bf16[512,512]{1,0:T(8,128)(2,1)S(1)} %collective-permute-done.3), channel_id=1, source_target_pairs={{0,32},{8,40},{16,48},{24,56},{32,64},{40,72},{48,80},{56,88},{64,... | collective-permute-start | bytes 1572872 | tf_op jit(solution)/shard_map/ppermute | solution.py:101
  45.1 14.6 %collective-permute-start.7 = (bf16[512,512]{1,0:T(8,128)(2,1)S(1)}, bf16[512,512]{1,0:T(8,128)(2,1)S(1)}, u32[]{:S(2)}, u32[]{:S(2)}) collective-permute-start(bf16[512,512]{1,0:T(8,128)(2,1)S(1)} %collective-permute-done.6), channel_id=1, source_target_pairs={{0,224},{8,232},{16,240},{24,248},{32,0},{40,8},{48,16},{56,24},{6... | collective-permute-start | bytes 1572872 | tf_op jit(solution)/shard_map/ppermute | solution.py:101
  58.8 12.9 %collective-permute-start.5 = (bf16[512,512]{1,0:T(8,128)(2,1)S(1)}, bf16[512,512]{1,0:T(8,128)(2,1)S(1)}, u32[]{:S(2)}, u32[]{:S(2)}) collective-permute-start(bf16[512,512]{1,0:T(8,128)(2,1)S(1)} %collective-permute-done.4), channel_id=1, source_target_pairs={{0,32},{8,40},{16,48},{24,56},{32,64},{40,72},{48,80},{56,88},{64,... | collective-permute-start | bytes 1572872 | tf_op jit(solution)/shard_map/ppermute | solution.py:101
  59.7 14.6 %collective-permute-start.8 = (bf16[512,512]{1,0:T(8,128)(2,1)S(1)}, bf16[512,512]{1,0:T(8,128)(2,1)S(1)}, u32[]{:S(2)}, u32[]{:S(2)}) collective-permute-start(bf16[512,512]{1,0:T(8,128)(2,1)S(1)} %collective-permute-done.7), channel_id=1, source_target_pairs={{0,224},{8,232},{16,240},{24,248},{32,0},{40,8},{48,16},{56,24},{6... | collective-permute-start | bytes 1572872 | tf_op jit(solution)/shard_map/ppermute | solution.py:101
  123.7 19.2 %all-to-all-start.1 = ((f32[8,1,32768]{2,1,0:T(1,128)}), f32[8,1,32768]{2,1,0:T(1,128)S(1)}, u32[]{:S(2)}, u32[]{:S(2)}) async-start(f32[8,1,32768]{2,1,0:T(1,128)} %broadcast_in_dim.39), calls=%async_computation.1 | async-start | bytes 2097152 | tf_op jit(solution)/shard_map/all_to_all | solution.py:42
  319.2 13.7 %collective-permute-start.20 = (f32[8,2,16,8192]{3,2,1,0:T(8,128)}, f32[8,2,16,8192]{3,2,1,0:T(8,128)}, u32[]{:S(2)}, u32[]{:S(2)}) collective-permute-start(f32[8,2,16,8192]{3,2,1,0:T(8,128)} %fusion), channel_id=1, source_target_pairs={{0,8},{8,0},{16,24},{24,16},{32,40},{40,32},{48,56},{56,48},{64,72... | collective-permute-start | bytes 25165832 | tf_op jit(solution)/shard_map/ppermute | solution.py:146
  334.2 10.5 %collective-permute-start.21 = (f32[8,8192]{1,0:T(8,128)S(1)}, f32[8,8192]{1,0:T(8,128)S(1)}, u32[]{:S(2)}, u32[]{:S(2)}) collective-permute-start(f32[8,8192]{1,0:T(8,128)S(1)} %get-tuple-element.35), channel_id=1, source_target_pairs={{0,32},{8,40},{16,48},{24,56},{32,64},{40,72},{48,80},{56,88},{64,... | collective-permute-start | bytes 786440 | tf_op jit(solution)/shard_map/ppermute | solution.py:160
  334.4 10.3 %collective-permute-start.42 = (f32[8,8192]{1,0:T(8,128)S(1)}, f32[8,8192]{1,0:T(8,128)S(1)}, u32[]{:S(2)}, u32[]{:S(2)}) collective-permute-start(f32[8,8192]{1,0:T(8,128)S(1)} %get-tuple-element.36), channel_id=1, source_target_pairs={{0,224},{8,232},{16,240},{24,248},{32,0},{40,8},{48,16},{56,24},{6... | collective-permute-start | bytes 786440 | tf_op jit(solution)/shard_map/ppermute | solution.py:160
  337.5 11.2 %collective-permute-start.35 = (f32[8,8192]{1,0:T(8,128)S(1)}, f32[8,8192]{1,0:T(8,128)S(1)}, u32[]{:S(2)}, u32[]{:S(2)}) collective-permute-start(f32[8,8192]{1,0:T(8,128)S(1)} %get-tuple-element.37), channel_id=1, source_target_pairs={{0,224},{8,232},{16,240},{24,248},{32,0},{40,8},{48,16},{56,24},{6... | collective-permute-start | bytes 786440 | tf_op jit(solution)/shard_map/ppermute | solution.py:160
  338.3 11.1 %collective-permute-start.28 = (f32[8,8192]{1,0:T(8,128)S(1)}, f32[8,8192]{1,0:T(8,128)S(1)}, u32[]{:S(2)}, u32[]{:S(2)}) collective-permute-start(f32[8,8192]{1,0:T(8,128)S(1)} %get-tuple-element.38), channel_id=1, source_target_pairs={{0,32},{8,40},{16,48},{24,56},{32,64},{40,72},{48,80},{56,88},{64,... | collective-permute-start | bytes 786440 | tf_op jit(solution)/shard_map/ppermute | solution.py:160
  351.1 10.5 %collective-permute-start.22 = (f32[8,8192]{1,0:T(8,128)S(1)}, f32[8,8192]{1,0:T(8,128)S(1)}, u32[]{:S(2)}, u32[]{:S(2)}) collective-permute-start(f32[8,8192]{1,0:T(8,128)S(1)} %get-tuple-element.31), channel_id=1, source_target_pairs={{0,32},{8,40},{16,48},{24,56},{32,64},{40,72},{48,80},{56,88},{64,... | collective-permute-start | bytes 786440 | tf_op jit(solution)/shard_map/ppermute | solution.py:160
  351.2 10.4 %collective-permute-start.43 = (f32[8,8192]{1,0:T(8,128)S(1)}, f32[8,8192]{1,0:T(8,128)S(1)}, u32[]{:S(2)}, u32[]{:S(2)}) collective-permute-start(f32[8,8192]{1,0:T(8,128)S(1)} %get-tuple-element.32), channel_id=1, source_target_pairs={{0,224},{8,232},{16,240},{24,248},{32,0},{40,8},{48,16},{56,24},{6... | collective-permute-start | bytes 786440 | tf_op jit(solution)/shard_map/ppermute | solution.py:160
  354.4 10.3 %collective-permute-start.36 = (f32[8,8192]{1,0:T(8,128)S(1)}, f32[8,8192]{1,0:T(8,128)S(1)}, u32[]{:S(2)}, u32[]{:S(2)}) collective-permute-start(f32[8,8192]{1,0:T(8,128)S(1)} %get-tuple-element.33), channel_id=1, source_target_pairs={{0,224},{8,232},{16,240},{24,248},{32,0},{40,8},{48,16},{56,24},{6... | collective-permute-start | bytes 786440 | tf_op jit(solution)/shard_map/ppermute | solution.py:160
  367.2 9.7 %collective-permute-start.23 = (f32[8,8192]{1,0:T(8,128)S(1)}, f32[8,8192]{1,0:T(8,128)S(1)}, u32[]{:S(2)}, u32[]{:S(2)}) collective-permute-start(f32[8,8192]{1,0:T(8,128)S(1)} %get-tuple-element.27), channel_id=1, source_target_pairs={{0,32},{8,40},{16,48},{24,56},{32,64},{40,72},{48,80},{56,88},{64,... | collective-permute-start | bytes 786440 | tf_op jit(solution)/shard_map/ppermute | solution.py:160
  370.5 9.7 %collective-permute-start.37 = (f32[8,8192]{1,0:T(8,128)S(1)}, f32[8,8192]{1,0:T(8,128)S(1)}, u32[]{:S(2)}, u32[]{:S(2)}) collective-permute-start(f32[8,8192]{1,0:T(8,128)S(1)} %get-tuple-element.29), channel_id=1, source_target_pairs={{0,224},{8,232},{16,240},{24,248},{32,0},{40,8},{48,16},{56,24},{6... | collective-permute-start | bytes 786440 | tf_op jit(solution)/shard_map/ppermute | solution.py:160
  382.4 10.3 %collective-permute-start.24 = (f32[8,8192]{1,0:T(8,128)S(1)}, f32[8,8192]{1,0:T(8,128)S(1)}, u32[]{:S(2)}, u32[]{:S(2)}) collective-permute-start(f32[8,8192]{1,0:T(8,128)S(1)} %get-tuple-element.23), channel_id=1, source_target_pairs={{0,32},{8,40},{16,48},{24,56},{32,64},{40,72},{48,80},{56,88},{64,... | collective-permute-start | bytes 786440 | tf_op jit(solution)/shard_map/ppermute | solution.py:160
  397.6 10.2 %collective-permute-start.25 = (f32[8,8192]{1,0:T(8,128)S(1)}, f32[8,8192]{1,0:T(8,128)S(1)}, u32[]{:S(2)}, u32[]{:S(2)}) collective-permute-start(f32[8,8192]{1,0:T(8,128)S(1)} %get-tuple-element.19), channel_id=1, source_target_pairs={{0,32},{8,40},{16,48},{24,56},{32,64},{40,72},{48,80},{56,88},{64,... | collective-permute-start | bytes 786440 | tf_op jit(solution)/shard_map/ppermute | solution.py:160
  412.5 9.9 %collective-permute-start.26 = (f32[8,8192]{1,0:T(8,128)S(1)}, f32[8,8192]{1,0:T(8,128)S(1)}, u32[]{:S(2)}, u32[]{:S(2)}) collective-permute-start(f32[8,8192]{1,0:T(8,128)S(1)} %get-tuple-element.15), channel_id=1, source_target_pairs={{0,32},{8,40},{16,48},{24,56},{32,64},{40,72},{48,80},{56,88},{64,... | collective-permute-start | bytes 786440 | tf_op jit(solution)/shard_map/ppermute | solution.py:160
  426.8 10.1 %collective-permute-start.27 = (f32[8,8192]{1,0:T(8,128)S(1)}, f32[8,8192]{1,0:T(8,128)S(1)}, u32[]{:S(2)}, u32[]{:S(2)}) collective-permute-start(f32[8,8192]{1,0:T(8,128)S(1)} %get-tuple-element.11), channel_id=1, source_target_pairs={{0,32},{8,40},{16,48},{24,56},{32,64},{40,72},{48,80},{56,88},{64,... | collective-permute-start | bytes 786440 | tf_op jit(solution)/shard_map/ppermute | solution.py:160
  427.1 9.8 %collective-permute-start.48 = (f32[8,8192]{1,0:T(8,128)S(1)}, f32[8,8192]{1,0:T(8,128)S(1)}, u32[]{:S(2)}, u32[]{:S(2)}) collective-permute-start(f32[8,8192]{1,0:T(8,128)S(1)} %get-tuple-element.12), channel_id=1, source_target_pairs={{0,224},{8,232},{16,240},{24,248},{32,0},{40,8},{48,16},{56,24},{6... | collective-permute-start | bytes 786440 | tf_op jit(solution)/shard_map/ppermute | solution.py:160
  441.4 10.8 %collective-permute-start.49 = (f32[16,8192]{1,0:T(8,128)S(1)}, f32[16,8192]{1,0:T(8,128)S(1)}, u32[]{:S(2)}, u32[]{:S(2)}) collective-permute-start(f32[16,8192]{1,0:T(8,128)S(1)} %fusion.37), channel_id=1, source_target_pairs={{0,16},{8,24},{16,0},{24,8},{32,48},{40,56},{48,32},{56,40},{64,80... | collective-permute-start | bytes 1572872 | tf_op jit(solution)/shard_map/ppermute | solution.py:167
  (38 other events, 320.6 us)

commit v3 on v2

--- a/solution.py
+++ b/solution.py
@@ -16,7 +16,7 @@
     return lax.ppermute(x, axis, perm)
 
 
-def all_reduce_halving(x, axis, size, bits):
+def all_reduce_halving(x, axis, size, bits, inner=None, inner_size=1):
     shape = x.shape
     x = x.reshape(-1)
     idx = lax.axis_index(axis)
@@ -26,6 +26,8 @@
         keep = lax.dynamic_index_in_dim(halves, mine, 0, keepdims=False)
         send = lax.dynamic_index_in_dim(halves, 1 - mine, 0, keepdims=False)
         x = keep + _swap(send, axis, size, bit)
+    if inner is not None:
+        x = all_reduce_a2a(x, inner, inner_size)
     for bit in reversed(bits):
         mine = (idx >> bit) & 1
         other = _swap(x, axis, size, bit)
@@ -121,7 +123,7 @@
     local_gram = jnp.dot(
         sketch.T, sketch, precision=HI, preferred_element_type=jnp.float32
     )
-    gram = all_reduce_halving(local_gram, RUN, runs, run_bits)
+    gram = all_reduce_halving(local_gram, RUN, runs, [0, 1], "z", runs // 4)
     inv = inverse_factor(gram)
     basis = jnp.dot(sketch, inv.T, precision=HI).astype(jnp.bfloat16)
     return reduce_scatter_projection(basis, gradients, runs)

time: 460 us -> 451 us (0.980)
  blocking collectives: 22.8 us -> 51.5 us
  waiting for transfers between devices: 195 us -> 167 us
  starting transfers between devices: 68 us -> 59.4 us
    ppermute x10 -> x4, waiting for transfers between devices: 45.7 us -> 17.3 us  [_swap(): return lax.ppermute(x, axis, perm)]
    all_to_all x1 -> x2, blocking collectives: 22.8 us -> 38.7 us  [all_reduce_a2a(): mine = jnp.sum(lax.all_to_all(blocks, axis, 0, 0), axis=0)]
    all_to_all x0 -> x1, blocking collectives: none -> 12.9 us  [all_reduce_a2a(): full = lax.all_to_all(jnp.broadcast_to(mine, blocks.shape), axis, 0, 0)]
    ppermute x10 -> x4, starting transfers between devices: 10.3 us -> 1.68 us  [_swap(): return lax.ppermute(x, axis, perm)]
  transfers between devices with their start and end apart: 51 -> 45, of which waited for: 42 -> 36; matrix products, arithmetic and copies ran while one was open for 3% -> 3% of each run, Pallas kernels for 0% -> 0%
where the time goes in v3:
time: 451 us; the launch traced here: 445 us
  waiting for transfers between devices  167 us (37%)
  other arithmetic  111 us (25%)
  starting transfers between devices  59.4 us (13%)
  blocking collectives  51.5 us (11%)
  matrix products  31.2 us (7%)
  local copies, waits for them, and re-layouts  23.7 us (5%)
    ppermute x28, waiting for transfers between devices, ring(): acc = lax.ppermute(part(d) if acc is None else acc + part(d), RUN, perm)  57.9 us
    another operation x12, other arithmetic, inverse_factor(): ljj = lax.linalg.cholesky(panel[:BLOCK], symmetrize_input=False)  49.7 us
    ppermute x7, waiting for transfers between devices, hops(): cur = lax.ppermute(cur, RUN, perm)  45.2 us
    another operation x8, other arithmetic, inverse_factor(): ijj = lax.linalg.triangular_solve(ljj, eye, left_side=True, lower=True)  42.2 us
    all_to_all x2, blocking collectives, all_reduce_a2a(): mine = jnp.sum(lax.all_to_all(blocks, axis, 0, 0), axis=0)  38.7 us
    ppermute x28, starting transfers between devices, ring(): acc = lax.ppermute(part(d) if acc is None else acc + part(d), RUN, perm)  37.6 us
    ppermute x4, waiting for transfers between devices, _swap(): return lax.ppermute(x, axis, perm)  17.3 us
    dot_general x2, matrix products, project(): lax.dot_general(b, gradients, (((0,), (0,)), ((), ())), preferred_element...  14.8 us
  transfers between devices with their start and end apart: 45, of which 36 were waited for; matrix products, arithmetic and copies ran while one was open for 3% of the time, Pallas kernels for 0%

profile of v3, /device:TPU:8, one launch (start us, length us, event | category | flops | bytes accessed | tf_op | source)
XLA Modules:
  0.0 444.6 jit_solution(11860360403826127622)
XLA Ops:
  1.5 6.8 %collective-permute-done = bf16[256,512]{1,0:T(8,128)(2,1)S(1)} collective-permute-done((bf16[256,512]{1,0:T(8,128)(2,1)}, bf16[256,512]{1,0:T(8,128)(2,1)S(1)}, u32[]{:S(2)}, u32[]{:S(2)}) %collective-permute-start) | collective-permute-done | bytes 262176 | tf_op jit(solution)/shard_map/ppermute | solution.py:92
  14.3 16.2 %collective-permute-done.2 = bf16[512,512]{1,0:T(8,128)(2,1)S(1)} collective-permute-done((bf16[512,512]{1,0:T(8,128)(2,1)S(1)}, bf16[512,512]{1,0:T(8,128)(2,1)S(1)}, u32[]{:S(2)}, u32[]{:S(2)}) %collective-permute-start.2) | collective-permute-done | bytes 524320 | tf_op jit(solution)/shard_map/ppermute | solution.py:103
  33.7 11.4 %collective-permute-done.3 = bf16[512,512]{1,0:T(8,128)(2,1)S(1)} collective-permute-done((bf16[512,512]{1,0:T(8,128)(2,1)S(1)}, bf16[512,512]{1,0:T(8,128)(2,1)S(1)}, u32[]{:S(2)}, u32[]{:S(2)}) %collective-permute-start.3) | collective-permute-done | bytes 524320 | tf_op jit(solution)/shard_map/ppermute | solution.py:103
  48.3 10.5 %collective-permute-done.4 = bf16[512,512]{1,0:T(8,128)(2,1)S(1)} collective-permute-done((bf16[512,512]{1,0:T(8,128)(2,1)S(1)}, bf16[512,512]{1,0:T(8,128)(2,1)S(1)}, u32[]{:S(2)}, u32[]{:S(2)}) %collective-permute-start.4) | collective-permute-done | bytes 524320 | tf_op jit(solution)/shard_map/ppermute | solution.py:103
  64.6 7.1 %collective-permute-done.5 = bf16[512,512]{1,0:T(8,128)(2,1)S(1)} collective-permute-done((bf16[512,512]{1,0:T(8,128)(2,1)S(1)}, bf16[512,512]{1,0:T(8,128)(2,1)S(1)}, u32[]{:S(2)}, u32[]{:S(2)}) %collective-permute-start.5) | collective-permute-done | bytes 524320 | tf_op jit(solution)/shard_map/ppermute | solution.py:103
  76.8 6.4 %collective-permute-done.9 = bf16[8,512,512]{2,1,0:T(8,128)(2,1)} collective-permute-done((bf16[8,512,512]{2,1,0:T(8,128)(2,1)}, bf16[8,512,512]{2,1,0:T(8,128)(2,1)}, u32[]{:S(2)}, u32[]{:S(2)}) %collective-permute-start.9) | collective-permute-done | bytes 4194336 | tf_op jit(solution)/shard_map/ppermute | solution.py:110
  98.7 22.8 %all_to_all.31 = f32[8,1,32768]{2,1,0:T(1,128)S(1)} all-to-all(f32[8,1,32768]{2,1,0:T(1,128)S(1)} %all_to_all.26), channel_id=1, replica_groups=mesh['z'=8,'xlo'=2,'core'=2,'xhi'=2,'y'=4] {'xhi','y'}, dimensions={0} | all-to-all | bytes 2097152 | tf_op jit(solution)/shard_map/all_to_all | solution.py:43
  129.3 13.4 %all-to-all-done.1 = f32[8,1,32768]{2,1,0:T(1,128)S(1)} async-done(((f32[8,1,32768]{2,1,0:T(1,128)}), f32[8,1,32768]{2,1,0:T(1,128)S(1)}, u32[]{:S(2)}, u32[]{:S(2)}) %all-to-all-start.1) | async-done | bytes 1048608 | tf_op jit(solution)/shard_map/all_to_all | solution.py:44
  152.7 7.7 %collective-permute-done.11 = f32[65536]{0:T(1024)S(1)} collective-permute-done((f32[65536]{0:T(1024)S(1)}, f32[65536]{0:T(1024)S(1)}, u32[]{:S(2)}, u32[]{:S(2)}) %collective-permute-start.11) | collective-permute-done | bytes 262176 | tf_op jit(solution)/shard_map/ppermute | solution.py:16
  160.4 15.8 %all_to_all.32 = f32[8,1,8192]{2,1,0:T(1,128)S(1)} all-to-all(f32[8,1,8192]{2,1,0:T(1,128)S(1)} %bitcast.231), channel_id=1, replica_groups=mesh['z'=8,'xlo'=2,'core'=2,'xhi'=2,'y'=4] {'z'}, dimensions={0} | all-to-all | bytes 524288 | tf_op jit(solution)/shard_map/all_to_all | solution.py:43
  176.6 12.9 %all_to_all.33 = f32[8,1,8192]{2,1,0:T(1,128)S(1)} all-to-all(f32[8,1,8192]{2,1,0:T(1,128)S(1)} %broadcast_in_dim.43), channel_id=1, replica_groups=mesh['z'=8,'xlo'=2,'core'=2,'xhi'=2,'y'=4] {'z'}, dimensions={0} | all-to-all | bytes 524288 | tf_op jit(solution)/shard_map/all_to_all | solution.py:44
  190.1 5.8 %collective-permute-done.12 = f32[65536]{0:T(1024)S(1)} collective-permute-done((f32[65536]{0:T(1024)S(1)}, f32[65536]{0:T(1024)S(1)}, u32[]{:S(2)}, u32[]{:S(2)}) %collective-permute-start.12) | collective-permute-done | bytes 262176 | tf_op jit(solution)/shard_map/ppermute | solution.py:16
  198.4 11.7 %custom-call.12 = f32[128,128]{1,0:T(8,128)S(1)} custom-call(f32[128,128]{1,0:T(8,128)S(1)} %slice.119), custom_call_target="Cholesky" | custom-call | tf_op jit(solution)/shard_map/cholesky/custom-call.1 | solution.py:61
  211.5 9.8 %custom-call.13 = f32[1,128,128]{1,2,0:T(8,128)S(1)} custom-call(f32[1,128,128]{2,1,0:T(8,128)S(1)} %fusion.67), custom_call_target="InvertDiagBlocksLowerTriangular" | custom-call | tf_op jit(solution)/shard_map/triangular_solve/custom-call.0 | solution.py:62
  222.6 11.7 %custom-call.14 = f32[128,128]{1,0:T(8,128)S(1)} custom-call(f32[128,128]{1,0:T(8,128)S(1)} %slice.123), custom_call_target="Cholesky" | custom-call | tf_op jit(solution)/shard_map/cholesky/custom-call.1 | solution.py:61
  235.7 10.2 %custom-call.15 = f32[1,128,128]{1,2,0:T(8,128)S(1)} custom-call(f32[1,128,128]{2,1,0:T(8,128)S(1)} %fusion.68), custom_call_target="InvertDiagBlocksLowerTriangular" | custom-call | tf_op jit(solution)/shard_map/triangular_solve/custom-call.0 | solution.py:62
  248.6 11.7 %custom-call.16 = f32[128,128]{1,0:T(8,128)S(1)} custom-call(f32[128,128]{1,0:T(8,128)S(1)} %slice.127), custom_call_target="Cholesky" | custom-call | tf_op jit(solution)/shard_map/cholesky/custom-call.1 | solution.py:61
  261.6 9.8 %custom-call.17 = f32[1,128,128]{1,2,0:T(8,128)S(1)} custom-call(f32[1,128,128]{2,1,0:T(8,128)S(1)} %fusion.69), custom_call_target="InvertDiagBlocksLowerTriangular" | custom-call | tf_op jit(solution)/shard_map/triangular_solve/custom-call.0 | solution.py:62
  273.0 11.9 %custom-call.18 = f32[128,128]{1,0:T(8,128)S(1)} custom-call(f32[128,128]{1,0:T(8,128)S(1)} %slice_subtract_fusion.2), custom_call_target="Cholesky" | custom-call | tf_op jit(solution)/shard_map/cholesky/custom-call.1 | solution.py:61
  286.2 9.8 %custom-call.19 = f32[1,128,128]{1,2,0:T(8,128)S(1)} custom-call(f32[1,128,128]{2,1,0:T(8,128)S(1)} %fusion.70), custom_call_target="InvertDiagBlocksLowerTriangular" | custom-call | tf_op jit(solution)/shard_map/triangular_solve/custom-call.0 | solution.py:62
  301.2 9.0 %fusion = f32[8,2,16,8192]{3,2,1,0:T(8,128)} fusion(bf16[512,8192]{1,0:T(8,128)(2,1)} %param.5, bf16[512,8,2,2,16]{0,4,3,2,1:T(8,128)(2,1)S(1)} %bitcast.234, s32[]{:T(128)S(6)} %select_n.416), kind=kOutput, calls=%fused_computation | convolution fusion | flops 2147483648 | bytes 17039364 | tf_op jit(solution)/shard_map/dot_general | solution.py:144
  310.6 5.7 %fusion.2 = f32[8,2,16,8192]{3,2,1,0:T(8,128)S(1)} fusion(bf16[512,8192]{1,0:T(8,128)(2,1)} %param.5, bf16[512,8,2,2,16]{0,4,3,2,1:T(8,128)(2,1)S(1)} %bitcast.235, s32[]{:T(128)S(6)} %select_n.412), kind=kOutput, calls=%fused_computation.2 | convolution fusion | flops 2147483648 | bytes 17039364 | tf_op jit(solution)/shard_map/dot_general | solution.py:144
  316.3 7.6 %collective-permute-done.14 = f32[8,2,16,8192]{3,2,1,0:T(8,128)} collective-permute-done((f32[8,2,16,8192]{3,2,1,0:T(8,128)}, f32[8,2,16,8192]{3,2,1,0:T(8,128)}, u32[]{:S(2)}, u32[]{:S(2)}) %collective-permute-start.14) | collective-permute-done | bytes 8388640 | tf_op jit(solution)/shard_map/ppermute | solution.py:148
  433.2 10.1 %collective-permute-done.43 = f32[16,8192]{1,0:T(8,128)S(1)} collective-permute-done((f32[16,8192]{1,0:T(8,128)S(1)}, f32[16,8192]{1,0:T(8,128)S(1)}, u32[]{:S(2)}, u32[]{:S(2)}) %collective-permute-start.43) | collective-permute-done | bytes 524320 | tf_op jit(solution)/shard_map/ppermute | solution.py:169
  (214 shorter events, 187.2 us)
Async XLA Ops:
  12.4 18.1 %collective-permute-start.2 = (bf16[512,512]{1,0:T(8,128)(2,1)S(1)}, bf16[512,512]{1,0:T(8,128)(2,1)S(1)}, u32[]{:S(2)}, u32[]{:S(2)}) collective-permute-start(bf16[512,512]{1,0:T(8,128)(2,1)S(1)} %get-tuple-element.43), channel_id=1, source_target_pairs={{0,32},{8,40},{16,48},{24,56},{32,64},{40,72},{48,80},{56,88},{64,... | collective-permute-start | bytes 1572872 | tf_op jit(solution)/shard_map/ppermute | solution.py:103
  30.4 14.6 %collective-permute-start.3 = (bf16[512,512]{1,0:T(8,128)(2,1)S(1)}, bf16[512,512]{1,0:T(8,128)(2,1)S(1)}, u32[]{:S(2)}, u32[]{:S(2)}) collective-permute-start(bf16[512,512]{1,0:T(8,128)(2,1)S(1)} %collective-permute-done.2), channel_id=1, source_target_pairs={{0,32},{8,40},{16,48},{24,56},{32,64},{40,72},{48,80},{56,88},{64,... | collective-permute-start | bytes 1572872 | tf_op jit(solution)/shard_map/ppermute | solution.py:103
  30.4 14.6 %collective-permute-start.6 = (bf16[512,512]{1,0:T(8,128)(2,1)S(1)}, bf16[512,512]{1,0:T(8,128)(2,1)S(1)}, u32[]{:S(2)}, u32[]{:S(2)}) collective-permute-start(bf16[512,512]{1,0:T(8,128)(2,1)S(1)} %get-tuple-element.43), channel_id=1, source_target_pairs={{0,224},{8,232},{16,240},{24,248},{32,0},{40,8},{48,16},{56,24},{6... | collective-permute-start | bytes 1572872 | tf_op jit(solution)/shard_map/ppermute | solution.py:103
  45.0 13.7 %collective-permute-start.4 = (bf16[512,512]{1,0:T(8,128)(2,1)S(1)}, bf16[512,512]{1,0:T(8,128)(2,1)S(1)}, u32[]{:S(2)}, u32[]{:S(2)}) collective-permute-start(bf16[512,512]{1,0:T(8,128)(2,1)S(1)} %collective-permute-done.3), channel_id=1, source_target_pairs={{0,32},{8,40},{16,48},{24,56},{32,64},{40,72},{48,80},{56,88},{64,... | collective-permute-start | bytes 1572872 | tf_op jit(solution)/shard_map/ppermute | solution.py:103
  45.1 14.7 %collective-permute-start.7 = (bf16[512,512]{1,0:T(8,128)(2,1)S(1)}, bf16[512,512]{1,0:T(8,128)(2,1)S(1)}, u32[]{:S(2)}, u32[]{:S(2)}) collective-permute-start(bf16[512,512]{1,0:T(8,128)(2,1)S(1)} %collective-permute-done.6), channel_id=1, source_target_pairs={{0,224},{8,232},{16,240},{24,248},{32,0},{40,8},{48,16},{56,24},{6... | collective-permute-start | bytes 1572872 | tf_op jit(solution)/shard_map/ppermute | solution.py:103
  58.8 12.9 %collective-permute-start.5 = (bf16[512,512]{1,0:T(8,128)(2,1)S(1)}, bf16[512,512]{1,0:T(8,128)(2,1)S(1)}, u32[]{:S(2)}, u32[]{:S(2)}) collective-permute-start(bf16[512,512]{1,0:T(8,128)(2,1)S(1)} %collective-permute-done.4), channel_id=1, source_target_pairs={{0,32},{8,40},{16,48},{24,56},{32,64},{40,72},{48,80},{56,88},{64,... | collective-permute-start | bytes 1572872 | tf_op jit(solution)/shard_map/ppermute | solution.py:103
  59.7 14.5 %collective-permute-start.8 = (bf16[512,512]{1,0:T(8,128)(2,1)S(1)}, bf16[512,512]{1,0:T(8,128)(2,1)S(1)}, u32[]{:S(2)}, u32[]{:S(2)}) collective-permute-start(bf16[512,512]{1,0:T(8,128)(2,1)S(1)} %collective-permute-done.7), channel_id=1, source_target_pairs={{0,224},{8,232},{16,240},{24,248},{32,0},{40,8},{48,16},{56,24},{6... | collective-permute-start | bytes 1572872 | tf_op jit(solution)/shard_map/ppermute | solution.py:103
  123.8 18.9 %all-to-all-start.1 = ((f32[8,1,32768]{2,1,0:T(1,128)}), f32[8,1,32768]{2,1,0:T(1,128)S(1)}, u32[]{:S(2)}, u32[]{:S(2)}) async-start(f32[8,1,32768]{2,1,0:T(1,128)} %broadcast_in_dim.42), calls=%async_computation.1 | async-start | bytes 2097152 | tf_op jit(solution)/shard_map/all_to_all | solution.py:44
  310.2 13.7 %collective-permute-start.14 = (f32[8,2,16,8192]{3,2,1,0:T(8,128)}, f32[8,2,16,8192]{3,2,1,0:T(8,128)}, u32[]{:S(2)}, u32[]{:S(2)}) collective-permute-start(f32[8,2,16,8192]{3,2,1,0:T(8,128)} %fusion), channel_id=1, source_target_pairs={{0,8},{8,0},{16,24},{24,16},{32,40},{40,32},{48,56},{56,48},{64,72... | collective-permute-start | bytes 25165832 | tf_op jit(solution)/shard_map/ppermute | solution.py:148
  325.3 10.5 %collective-permute-start.15 = (f32[8,8192]{1,0:T(8,128)S(1)}, f32[8,8192]{1,0:T(8,128)S(1)}, u32[]{:S(2)}, u32[]{:S(2)}) collective-permute-start(f32[8,8192]{1,0:T(8,128)S(1)} %get-tuple-element.35), channel_id=1, source_target_pairs={{0,32},{8,40},{16,48},{24,56},{32,64},{40,72},{48,80},{56,88},{64,... | collective-permute-start | bytes 786440 | tf_op jit(solution)/shard_map/ppermute | solution.py:162
  328.6 11.2 %collective-permute-start.29 = (f32[8,8192]{1,0:T(8,128)S(1)}, f32[8,8192]{1,0:T(8,128)S(1)}, u32[]{:S(2)}, u32[]{:S(2)}) collective-permute-start(f32[8,8192]{1,0:T(8,128)S(1)} %get-tuple-element.37), channel_id=1, source_target_pairs={{0,224},{8,232},{16,240},{24,248},{32,0},{40,8},{48,16},{56,24},{6... | collective-permute-start | bytes 786440 | tf_op jit(solution)/shard_map/ppermute | solution.py:162
  328.6 11.9 %collective-permute-start.22 = (f32[8,8192]{1,0:T(8,128)S(1)}, f32[8,8192]{1,0:T(8,128)S(1)}, u32[]{:S(2)}, u32[]{:S(2)}) collective-permute-start(f32[8,8192]{1,0:T(8,128)S(1)} %get-tuple-element.38), channel_id=1, source_target_pairs={{0,32},{8,40},{16,48},{24,56},{32,64},{40,72},{48,80},{56,88},{64,... | collective-permute-start | bytes 786440 | tf_op jit(solution)/shard_map/ppermute | solution.py:162
  342.2 10.5 %collective-permute-start.16 = (f32[8,8192]{1,0:T(8,128)S(1)}, f32[8,8192]{1,0:T(8,128)S(1)}, u32[]{:S(2)}, u32[]{:S(2)}) collective-permute-start(f32[8,8192]{1,0:T(8,128)S(1)} %get-tuple-element.31), channel_id=1, source_target_pairs={{0,32},{8,40},{16,48},{24,56},{32,64},{40,72},{48,80},{56,88},{64,... | collective-permute-start | bytes 786440 | tf_op jit(solution)/shard_map/ppermute | solution.py:162
  342.3 10.4 %collective-permute-start.37 = (f32[8,8192]{1,0:T(8,128)S(1)}, f32[8,8192]{1,0:T(8,128)S(1)}, u32[]{:S(2)}, u32[]{:S(2)}) collective-permute-start(f32[8,8192]{1,0:T(8,128)S(1)} %get-tuple-element.32), channel_id=1, source_target_pairs={{0,224},{8,232},{16,240},{24,248},{32,0},{40,8},{48,16},{56,24},{6... | collective-permute-start | bytes 786440 | tf_op jit(solution)/shard_map/ppermute | solution.py:162
  345.5 10.3 %collective-permute-start.30 = (f32[8,8192]{1,0:T(8,128)S(1)}, f32[8,8192]{1,0:T(8,128)S(1)}, u32[]{:S(2)}, u32[]{:S(2)}) collective-permute-start(f32[8,8192]{1,0:T(8,128)S(1)} %get-tuple-element.33), channel_id=1, source_target_pairs={{0,224},{8,232},{16,240},{24,248},{32,0},{40,8},{48,16},{56,24},{6... | collective-permute-start | bytes 786440 | tf_op jit(solution)/shard_map/ppermute | solution.py:162
  358.3 9.9 %collective-permute-start.38 = (f32[8,8192]{1,0:T(8,128)S(1)}, f32[8,8192]{1,0:T(8,128)S(1)}, u32[]{:S(2)}, u32[]{:S(2)}) collective-permute-start(f32[8,8192]{1,0:T(8,128)S(1)} %get-tuple-element.28), channel_id=1, source_target_pairs={{0,224},{8,232},{16,240},{24,248},{32,0},{40,8},{48,16},{56,24},{6... | collective-permute-start | bytes 786440 | tf_op jit(solution)/shard_map/ppermute | solution.py:162
  373.4 10.3 %collective-permute-start.18 = (f32[8,8192]{1,0:T(8,128)S(1)}, f32[8,8192]{1,0:T(8,128)S(1)}, u32[]{:S(2)}, u32[]{:S(2)}) collective-permute-start(f32[8,8192]{1,0:T(8,128)S(1)} %get-tuple-element.23), channel_id=1, source_target_pairs={{0,32},{8,40},{16,48},{24,56},{32,64},{40,72},{48,80},{56,88},{64,... | collective-permute-start | bytes 786440 | tf_op jit(solution)/shard_map/ppermute | solution.py:162
  373.8 10.0 %collective-permute-start.39 = (f32[8,8192]{1,0:T(8,128)S(1)}, f32[8,8192]{1,0:T(8,128)S(1)}, u32[]{:S(2)}, u32[]{:S(2)}) collective-permute-start(f32[8,8192]{1,0:T(8,128)S(1)} %get-tuple-element.24), channel_id=1, source_target_pairs={{0,224},{8,232},{16,240},{24,248},{32,0},{40,8},{48,16},{56,24},{6... | collective-permute-start | bytes 786440 | tf_op jit(solution)/shard_map/ppermute | solution.py:162
  388.6 10.2 %collective-permute-start.19 = (f32[8,8192]{1,0:T(8,128)S(1)}, f32[8,8192]{1,0:T(8,128)S(1)}, u32[]{:S(2)}, u32[]{:S(2)}) collective-permute-start(f32[8,8192]{1,0:T(8,128)S(1)} %get-tuple-element.19), channel_id=1, source_target_pairs={{0,32},{8,40},{16,48},{24,56},{32,64},{40,72},{48,80},{56,88},{64,... | collective-permute-start | bytes 786440 | tf_op jit(solution)/shard_map/ppermute | solution.py:162
  388.7 10.1 %collective-permute-start.40 = (f32[8,8192]{1,0:T(8,128)S(1)}, f32[8,8192]{1,0:T(8,128)S(1)}, u32[]{:S(2)}, u32[]{:S(2)}) collective-permute-start(f32[8,8192]{1,0:T(8,128)S(1)} %get-tuple-element.20), channel_id=1, source_target_pairs={{0,224},{8,232},{16,240},{24,248},{32,0},{40,8},{48,16},{56,24},{6... | collective-permute-start | bytes 786440 | tf_op jit(solution)/shard_map/ppermute | solution.py:162
  403.6 9.9 %collective-permute-start.20 = (f32[8,8192]{1,0:T(8,128)S(1)}, f32[8,8192]{1,0:T(8,128)S(1)}, u32[]{:S(2)}, u32[]{:S(2)}) collective-permute-start(f32[8,8192]{1,0:T(8,128)S(1)} %get-tuple-element.15), channel_id=1, source_target_pairs={{0,32},{8,40},{16,48},{24,56},{32,64},{40,72},{48,80},{56,88},{64,... | collective-permute-start | bytes 786440 | tf_op jit(solution)/shard_map/ppermute | solution.py:162
  417.9 10.1 %collective-permute-start.21 = (f32[8,8192]{1,0:T(8,128)S(1)}, f32[8,8192]{1,0:T(8,128)S(1)}, u32[]{:S(2)}, u32[]{:S(2)}) collective-permute-start(f32[8,8192]{1,0:T(8,128)S(1)} %get-tuple-element.11), channel_id=1, source_target_pairs={{0,32},{8,40},{16,48},{24,56},{32,64},{40,72},{48,80},{56,88},{64,... | collective-permute-start | bytes 786440 | tf_op jit(solution)/shard_map/ppermute | solution.py:162
  418.0 10.0 %collective-permute-start.42 = (f32[8,8192]{1,0:T(8,128)S(1)}, f32[8,8192]{1,0:T(8,128)S(1)}, u32[]{:S(2)}, u32[]{:S(2)}) collective-permute-start(f32[8,8192]{1,0:T(8,128)S(1)} %get-tuple-element.12), channel_id=1, source_target_pairs={{0,224},{8,232},{16,240},{24,248},{32,0},{40,8},{48,16},{56,24},{6... | collective-permute-start | bytes 786440 | tf_op jit(solution)/shard_map/ppermute | solution.py:162
  432.5 10.8 %collective-permute-start.43 = (f32[16,8192]{1,0:T(8,128)S(1)}, f32[16,8192]{1,0:T(8,128)S(1)}, u32[]{:S(2)}, u32[]{:S(2)}) collective-permute-start(f32[16,8192]{1,0:T(8,128)S(1)} %fusion.37), channel_id=1, source_target_pairs={{0,16},{8,24},{16,0},{24,8},{32,48},{40,56},{48,32},{56,40},{64,80... | collective-permute-start | bytes 1572872 | tf_op jit(solution)/shard_map/ppermute | solution.py:169
  (32 other events, 285.7 us)

commit v4 on v3

--- a/solution.py
+++ b/solution.py
@@ -119,7 +119,7 @@
 def per_device(runs, entries, gradients, probes):
     run_bits = list(range(runs.bit_length() - 1))
     partial_sketch = gathered_sketch(gradients, probes, runs)
-    sketch = all_reduce_a2a(partial_sketch, ENTRY, entries)
+    sketch = all_reduce_halving(partial_sketch, ENTRY, entries, [(entries // 2).bit_length() - 1], "y", entries // 2)
     local_gram = jnp.dot(
         sketch.T, sketch, precision=HI, preferred_element_type=jnp.float32
     )

time: 451 us -> 457 us (1.013)
  waiting for transfers between devices: 167 us -> 172 us
    ppermute x4 -> x6, waiting for transfers between devices: 17.3 us -> 37 us  [_swap(): return lax.ppermute(x, axis, perm)]
    all_to_all x1 -> x0, waiting for transfers between devices: 13.4 us -> none  [all_reduce_a2a(): full = lax.all_to_all(jnp.broadcast_to(mine, blocks.shape), axis, 0, 0)]
    all_to_all x2, blocking collectives: 38.7 us -> 28 us  [all_reduce_a2a(): mine = jnp.sum(lax.all_to_all(blocks, axis, 0, 0), axis=0)]
    all_to_all x1 -> x2, blocking collectives: 12.9 us -> 23.4 us  [all_reduce_a2a(): full = lax.all_to_all(jnp.broadcast_to(mine, blocks.shape), axis, 0, 0)]
    ppermute x4 -> x6, starting transfers between devices: 1.68 us -> 9.76 us  [_swap(): return lax.ppermute(x, axis, perm)]
    all_to_all x1 -> x0, starting transfers between devices: 5.47 us -> none  [all_reduce_a2a(): full = lax.all_to_all(jnp.broadcast_to(mine, blocks.shape), axis, 0, 0)]
  transfers between devices with their start and end apart: 45 -> 46, of which waited for: 36 -> 37; matrix products, arithmetic and copies ran while one was open for 3% -> 3% of each run, Pallas kernels for 0% -> 0%
where the time goes in v4:
time: 457 us; the launch traced here: 450 us
  waiting for transfers between devices  172 us (38%)
  other arithmetic  108 us (24%)
  starting transfers between devices  62.9 us (14%)
  blocking collectives  51.4 us (11%)
  matrix products  31.2 us (7%)
  local copies, waits for them, and re-layouts  23 us (5%)
    ppermute x28, waiting for transfers between devices, ring(): acc = lax.ppermute(part(d) if acc is None else acc + part(d), RUN, perm)  57.9 us
    another operation x12, other arithmetic, inverse_factor(): ljj = lax.linalg.cholesky(panel[:BLOCK], symmetrize_input=False)  49.7 us
    ppermute x7, waiting for transfers between devices, hops(): cur = lax.ppermute(cur, RUN, perm)  45.1 us
    another operation x8, other arithmetic, inverse_factor(): ijj = lax.linalg.triangular_solve(ljj, eye, left_side=True, lower=True)  42.2 us
    ppermute x28, starting transfers between devices, ring(): acc = lax.ppermute(part(d) if acc is None else acc + part(d), RUN, perm)  37.6 us
    ppermute x6, waiting for transfers between devices, _swap(): return lax.ppermute(x, axis, perm)  37 us
    all_to_all x2, blocking collectives, all_reduce_a2a(): mine = jnp.sum(lax.all_to_all(blocks, axis, 0, 0), axis=0)  28 us
    all_to_all x2, blocking collectives, all_reduce_a2a(): full = lax.all_to_all(jnp.broadcast_to(mine, blocks.shape), axis, 0, 0)  23.4 us
  transfers between devices with their start and end apart: 46, of which 37 were waited for; matrix products, arithmetic and copies ran while one was open for 3% of the time, Pallas kernels for 0%

profile of v4, /device:TPU:8, one launch (start us, length us, event | category | flops | bytes accessed | tf_op | source)
XLA Modules:
  0.0 450.1 jit_solution(6785948379172311612)
XLA Ops:
  1.5 6.8 %collective-permute-done = bf16[256,512]{1,0:T(8,128)(2,1)S(1)} collective-permute-done((bf16[256,512]{1,0:T(8,128)(2,1)}, bf16[256,512]{1,0:T(8,128)(2,1)S(1)}, u32[]{:S(2)}, u32[]{:S(2)}) %collective-permute-start) | collective-permute-done | bytes 262176 | tf_op jit(solution)/shard_map/ppermute | solution.py:92
  14.3 16.2 %collective-permute-done.2 = bf16[512,512]{1,0:T(8,128)(2,1)S(1)} collective-permute-done((bf16[512,512]{1,0:T(8,128)(2,1)S(1)}, bf16[512,512]{1,0:T(8,128)(2,1)S(1)}, u32[]{:S(2)}, u32[]{:S(2)}) %collective-permute-start.2) | collective-permute-done | bytes 524320 | tf_op jit(solution)/shard_map/ppermute | solution.py:103
  33.7 11.4 %collective-permute-done.3 = bf16[512,512]{1,0:T(8,128)(2,1)S(1)} collective-permute-done((bf16[512,512]{1,0:T(8,128)(2,1)S(1)}, bf16[512,512]{1,0:T(8,128)(2,1)S(1)}, u32[]{:S(2)}, u32[]{:S(2)}) %collective-permute-start.3) | collective-permute-done | bytes 524320 | tf_op jit(solution)/shard_map/ppermute | solution.py:103
  48.3 10.5 %collective-permute-done.4 = bf16[512,512]{1,0:T(8,128)(2,1)S(1)} collective-permute-done((bf16[512,512]{1,0:T(8,128)(2,1)S(1)}, bf16[512,512]{1,0:T(8,128)(2,1)S(1)}, u32[]{:S(2)}, u32[]{:S(2)}) %collective-permute-start.4) | collective-permute-done | bytes 524320 | tf_op jit(solution)/shard_map/ppermute | solution.py:103
  64.6 7.1 %collective-permute-done.5 = bf16[512,512]{1,0:T(8,128)(2,1)S(1)} collective-permute-done((bf16[512,512]{1,0:T(8,128)(2,1)S(1)}, bf16[512,512]{1,0:T(8,128)(2,1)S(1)}, u32[]{:S(2)}, u32[]{:S(2)}) %collective-permute-start.5) | collective-permute-done | bytes 524320 | tf_op jit(solution)/shard_map/ppermute | solution.py:103
  76.8 6.4 %collective-permute-done.9 = bf16[8,512,512]{2,1,0:T(8,128)(2,1)} collective-permute-done((bf16[8,512,512]{2,1,0:T(8,128)(2,1)}, bf16[8,512,512]{2,1,0:T(8,128)(2,1)}, u32[]{:S(2)}, u32[]{:S(2)}) %collective-permute-start.9) | collective-permute-done | bytes 4194336 | tf_op jit(solution)/shard_map/ppermute | solution.py:110
  102.4 12.4 %collective-permute-done.10 = f32[131072]{0:T(1024)S(1)} collective-permute-done((f32[131072]{0:T(1024)S(1)}, f32[131072]{0:T(1024)S(1)}, u32[]{:S(2)}, u32[]{:S(2)}) %collective-permute-start.10) | collective-permute-done | bytes 524320 | tf_op jit(solution)/shard_map/ppermute | solution.py:16
  114.9 12.2 %all_to_all.30 = f32[4,1,32768]{2,1,0:T(1,128)S(1)} all-to-all(f32[4,1,32768]{2,1,0:T(1,128)S(1)} %bitcast.235), channel_id=1, replica_groups=mesh['z'=8,'xlo'=2,'core'=2,'xhi'=2,'y'=4] {'y'}, dimensions={0} | all-to-all | bytes 1048576 | tf_op jit(solution)/shard_map/all_to_all | solution.py:43
  127.8 10.5 %all_to_all.31 = f32[4,1,32768]{2,1,0:T(1,128)S(1)} all-to-all(f32[4,1,32768]{2,1,0:T(1,128)S(1)} %broadcast_in_dim.42), channel_id=1, replica_groups=mesh['z'=8,'xlo'=2,'core'=2,'xhi'=2,'y'=4] {'y'}, dimensions={0} | all-to-all | bytes 1048576 | tf_op jit(solution)/shard_map/all_to_all | solution.py:44
  141.5 9.0 %collective-permute-done.11 = f32[131072]{0:T(1024)S(1)} collective-permute-done((f32[131072]{0:T(1024)S(1)}, f32[131072]{0:T(1024)S(1)}, u32[]{:S(2)}, u32[]{:S(2)}) %collective-permute-start.11) | collective-permute-done | bytes 524320 | tf_op jit(solution)/shard_map/ppermute | solution.py:16
  159.0 6.9 %collective-permute-done.13 = f32[65536]{0:T(1024)S(1)} collective-permute-done((f32[65536]{0:T(1024)S(1)}, f32[65536]{0:T(1024)S(1)}, u32[]{:S(2)}, u32[]{:S(2)}) %collective-permute-start.13) | collective-permute-done | bytes 262176 | tf_op jit(solution)/shard_map/ppermute | solution.py:16
  165.9 15.8 %all_to_all.32 = f32[8,1,8192]{2,1,0:T(1,128)S(1)} all-to-all(f32[8,1,8192]{2,1,0:T(1,128)S(1)} %bitcast.239), channel_id=1, replica_groups=mesh['z'=8,'xlo'=2,'core'=2,'xhi'=2,'y'=4] {'z'}, dimensions={0} | all-to-all | bytes 524288 | tf_op jit(solution)/shard_map/all_to_all | solution.py:43
  182.1 12.9 %all_to_all.33 = f32[8,1,8192]{2,1,0:T(1,128)S(1)} all-to-all(f32[8,1,8192]{2,1,0:T(1,128)S(1)} %broadcast_in_dim.43), channel_id=1, replica_groups=mesh['z'=8,'xlo'=2,'core'=2,'xhi'=2,'y'=4] {'z'}, dimensions={0} | all-to-all | bytes 524288 | tf_op jit(solution)/shard_map/all_to_all | solution.py:44
  203.8 11.7 %custom-call.12 = f32[128,128]{1,0:T(8,128)S(1)} custom-call(f32[128,128]{1,0:T(8,128)S(1)} %slice.119), custom_call_target="Cholesky" | custom-call | tf_op jit(solution)/shard_map/cholesky/custom-call.1 | solution.py:61
  216.9 9.8 %custom-call.13 = f32[1,128,128]{1,2,0:T(8,128)S(1)} custom-call(f32[1,128,128]{2,1,0:T(8,128)S(1)} %fusion.67), custom_call_target="InvertDiagBlocksLowerTriangular" | custom-call | tf_op jit(solution)/shard_map/triangular_solve/custom-call.0 | solution.py:62
  228.1 11.7 %custom-call.14 = f32[128,128]{1,0:T(8,128)S(1)} custom-call(f32[128,128]{1,0:T(8,128)S(1)} %slice.123), custom_call_target="Cholesky" | custom-call | tf_op jit(solution)/shard_map/cholesky/custom-call.1 | solution.py:61
  241.1 10.2 %custom-call.15 = f32[1,128,128]{1,2,0:T(8,128)S(1)} custom-call(f32[1,128,128]{2,1,0:T(8,128)S(1)} %fusion.68), custom_call_target="InvertDiagBlocksLowerTriangular" | custom-call | tf_op jit(solution)/shard_map/triangular_solve/custom-call.0 | solution.py:62
  254.0 11.7 %custom-call.16 = f32[128,128]{1,0:T(8,128)S(1)} custom-call(f32[128,128]{1,0:T(8,128)S(1)} %slice.127), custom_call_target="Cholesky" | custom-call | tf_op jit(solution)/shard_map/cholesky/custom-call.1 | solution.py:61
  267.0 9.8 %custom-call.17 = f32[1,128,128]{1,2,0:T(8,128)S(1)} custom-call(f32[1,128,128]{2,1,0:T(8,128)S(1)} %fusion.69), custom_call_target="InvertDiagBlocksLowerTriangular" | custom-call | tf_op jit(solution)/shard_map/triangular_solve/custom-call.0 | solution.py:62
  278.4 11.9 %custom-call.18 = f32[128,128]{1,0:T(8,128)S(1)} custom-call(f32[128,128]{1,0:T(8,128)S(1)} %slice_subtract_fusion.2), custom_call_target="Cholesky" | custom-call | tf_op jit(solution)/shard_map/cholesky/custom-call.1 | solution.py:61
  291.6 9.8 %custom-call.19 = f32[1,128,128]{1,2,0:T(8,128)S(1)} custom-call(f32[1,128,128]{2,1,0:T(8,128)S(1)} %fusion.70), custom_call_target="InvertDiagBlocksLowerTriangular" | custom-call | tf_op jit(solution)/shard_map/triangular_solve/custom-call.0 | solution.py:62
  306.6 9.0 %fusion = f32[8,2,16,8192]{3,2,1,0:T(8,128)} fusion(bf16[512,8192]{1,0:T(8,128)(2,1)} %param.5, bf16[512,8,2,2,16]{0,4,3,2,1:T(8,128)(2,1)S(1)} %bitcast.242, s32[]{:T(128)S(6)} %select_n.437), kind=kOutput, calls=%fused_computation | convolution fusion | flops 2147483648 | bytes 17039364 | tf_op jit(solution)/shard_map/dot_general | solution.py:144
  321.7 7.6 %collective-permute-done.16 = f32[8,2,16,8192]{3,2,1,0:T(8,128)} collective-permute-done((f32[8,2,16,8192]{3,2,1,0:T(8,128)}, f32[8,2,16,8192]{3,2,1,0:T(8,128)}, u32[]{:S(2)}, u32[]{:S(2)}) %collective-permute-start.16) | collective-permute-done | bytes 8388640 | tf_op jit(solution)/shard_map/ppermute | solution.py:148
  439.5 9.2 %collective-permute-done.45 = f32[16,8192]{1,0:T(8,128)S(1)} collective-permute-done((f32[16,8192]{1,0:T(8,128)S(1)}, f32[16,8192]{1,0:T(8,128)S(1)}, u32[]{:S(2)}, u32[]{:S(2)}) %collective-permute-start.45) | collective-permute-done | bytes 524320 | tf_op jit(solution)/shard_map/ppermute | solution.py:169
  (222 shorter events, 198.0 us)
Async XLA Ops:
  12.4 18.1 %collective-permute-start.2 = (bf16[512,512]{1,0:T(8,128)(2,1)S(1)}, bf16[512,512]{1,0:T(8,128)(2,1)S(1)}, u32[]{:S(2)}, u32[]{:S(2)}) collective-permute-start(bf16[512,512]{1,0:T(8,128)(2,1)S(1)} %get-tuple-element.47), channel_id=1, source_target_pairs={{0,32},{8,40},{16,48},{24,56},{32,64},{40,72},{48,80},{56,88},{64,... | collective-permute-start | bytes 1572872 | tf_op jit(solution)/shard_map/ppermute | solution.py:103
  30.4 14.6 %collective-permute-start.3 = (bf16[512,512]{1,0:T(8,128)(2,1)S(1)}, bf16[512,512]{1,0:T(8,128)(2,1)S(1)}, u32[]{:S(2)}, u32[]{:S(2)}) collective-permute-start(bf16[512,512]{1,0:T(8,128)(2,1)S(1)} %collective-permute-done.2), channel_id=1, source_target_pairs={{0,32},{8,40},{16,48},{24,56},{32,64},{40,72},{48,80},{56,88},{64,... | collective-permute-start | bytes 1572872 | tf_op jit(solution)/shard_map/ppermute | solution.py:103
  30.4 14.6 %collective-permute-start.6 = (bf16[512,512]{1,0:T(8,128)(2,1)S(1)}, bf16[512,512]{1,0:T(8,128)(2,1)S(1)}, u32[]{:S(2)}, u32[]{:S(2)}) collective-permute-start(bf16[512,512]{1,0:T(8,128)(2,1)S(1)} %get-tuple-element.47), channel_id=1, source_target_pairs={{0,224},{8,232},{16,240},{24,248},{32,0},{40,8},{48,16},{56,24},{6... | collective-permute-start | bytes 1572872 | tf_op jit(solution)/shard_map/ppermute | solution.py:103
  45.0 13.7 %collective-permute-start.4 = (bf16[512,512]{1,0:T(8,128)(2,1)S(1)}, bf16[512,512]{1,0:T(8,128)(2,1)S(1)}, u32[]{:S(2)}, u32[]{:S(2)}) collective-permute-start(bf16[512,512]{1,0:T(8,128)(2,1)S(1)} %collective-permute-done.3), channel_id=1, source_target_pairs={{0,32},{8,40},{16,48},{24,56},{32,64},{40,72},{48,80},{56,88},{64,... | collective-permute-start | bytes 1572872 | tf_op jit(solution)/shard_map/ppermute | solution.py:103
  45.1 14.7 %collective-permute-start.7 = (bf16[512,512]{1,0:T(8,128)(2,1)S(1)}, bf16[512,512]{1,0:T(8,128)(2,1)S(1)}, u32[]{:S(2)}, u32[]{:S(2)}) collective-permute-start(bf16[512,512]{1,0:T(8,128)(2,1)S(1)} %collective-permute-done.6), channel_id=1, source_target_pairs={{0,224},{8,232},{16,240},{24,248},{32,0},{40,8},{48,16},{56,24},{6... | collective-permute-start | bytes 1572872 | tf_op jit(solution)/shard_map/ppermute | solution.py:103
  58.8 12.9 %collective-permute-start.5 = (bf16[512,512]{1,0:T(8,128)(2,1)S(1)}, bf16[512,512]{1,0:T(8,128)(2,1)S(1)}, u32[]{:S(2)}, u32[]{:S(2)}) collective-permute-start(bf16[512,512]{1,0:T(8,128)(2,1)S(1)} %collective-permute-done.4), channel_id=1, source_target_pairs={{0,32},{8,40},{16,48},{24,56},{32,64},{40,72},{48,80},{56,88},{64,... | collective-permute-start | bytes 1572872 | tf_op jit(solution)/shard_map/ppermute | solution.py:103
  59.7 14.6 %collective-permute-start.8 = (bf16[512,512]{1,0:T(8,128)(2,1)S(1)}, bf16[512,512]{1,0:T(8,128)(2,1)S(1)}, u32[]{:S(2)}, u32[]{:S(2)}) collective-permute-start(bf16[512,512]{1,0:T(8,128)(2,1)S(1)} %collective-permute-done.7), channel_id=1, source_target_pairs={{0,224},{8,232},{16,240},{24,248},{32,0},{40,8},{48,16},{56,24},{6... | collective-permute-start | bytes 1572872 | tf_op jit(solution)/shard_map/ppermute | solution.py:103
  99.3 15.6 %collective-permute-start.10 = (f32[131072]{0:T(1024)S(1)}, f32[131072]{0:T(1024)S(1)}, u32[]{:S(2)}, u32[]{:S(2)}) collective-permute-start(f32[131072]{0:T(1024)S(1)} %bitcast.245), channel_id=1, source_target_pairs={{0,4},{1,5},{2,6},{3,7},{4,0},{5,1},{6,2},{7,3},{8,12},{9,13},{10,... | collective-permute-start | bytes 1572872 | tf_op jit(solution)/shard_map/ppermute | solution.py:16
  138.3 12.2 %collective-permute-start.11 = (f32[131072]{0:T(1024)S(1)}, f32[131072]{0:T(1024)S(1)}, u32[]{:S(2)}, u32[]{:S(2)}) collective-permute-start(f32[131072]{0:T(1024)S(1)} %bitcast.233), channel_id=1, source_target_pairs={{0,4},{1,5},{2,6},{3,7},{4,0},{5,1},{6,2},{7,3},{8,12},{9,13},{10,... | collective-permute-start | bytes 1572872 | tf_op jit(solution)/shard_map/ppermute | solution.py:16
  315.7 13.7 %collective-permute-start.16 = (f32[8,2,16,8192]{3,2,1,0:T(8,128)}, f32[8,2,16,8192]{3,2,1,0:T(8,128)}, u32[]{:S(2)}, u32[]{:S(2)}) collective-permute-start(f32[8,2,16,8192]{3,2,1,0:T(8,128)} %fusion), channel_id=1, source_target_pairs={{0,8},{8,0},{16,24},{24,16},{32,40},{40,32},{48,56},{56,48},{64,72... | collective-permute-start | bytes 25165832 | tf_op jit(solution)/shard_map/ppermute | solution.py:148
  330.7 10.5 %collective-permute-start.17 = (f32[8,8192]{1,0:T(8,128)S(1)}, f32[8,8192]{1,0:T(8,128)S(1)}, u32[]{:S(2)}, u32[]{:S(2)}) collective-permute-start(f32[8,8192]{1,0:T(8,128)S(1)} %get-tuple-element.35), channel_id=1, source_target_pairs={{0,32},{8,40},{16,48},{24,56},{32,64},{40,72},{48,80},{56,88},{64,... | collective-permute-start | bytes 786440 | tf_op jit(solution)/shard_map/ppermute | solution.py:162
  334.0 11.2 %collective-permute-start.31 = (f32[8,8192]{1,0:T(8,128)S(1)}, f32[8,8192]{1,0:T(8,128)S(1)}, u32[]{:S(2)}, u32[]{:S(2)}) collective-permute-start(f32[8,8192]{1,0:T(8,128)S(1)} %get-tuple-element.37), channel_id=1, source_target_pairs={{0,224},{8,232},{16,240},{24,248},{32,0},{40,8},{48,16},{56,24},{6... | collective-permute-start | bytes 786440 | tf_op jit(solution)/shard_map/ppermute | solution.py:162
  334.0 11.9 %collective-permute-start.24 = (f32[8,8192]{1,0:T(8,128)S(1)}, f32[8,8192]{1,0:T(8,128)S(1)}, u32[]{:S(2)}, u32[]{:S(2)}) collective-permute-start(f32[8,8192]{1,0:T(8,128)S(1)} %get-tuple-element.38), channel_id=1, source_target_pairs={{0,32},{8,40},{16,48},{24,56},{32,64},{40,72},{48,80},{56,88},{64,... | collective-permute-start | bytes 786440 | tf_op jit(solution)/shard_map/ppermute | solution.py:162
  347.6 10.5 %collective-permute-start.18 = (f32[8,8192]{1,0:T(8,128)S(1)}, f32[8,8192]{1,0:T(8,128)S(1)}, u32[]{:S(2)}, u32[]{:S(2)}) collective-permute-start(f32[8,8192]{1,0:T(8,128)S(1)} %get-tuple-element.31), channel_id=1, source_target_pairs={{0,32},{8,40},{16,48},{24,56},{32,64},{40,72},{48,80},{56,88},{64,... | collective-permute-start | bytes 786440 | tf_op jit(solution)/shard_map/ppermute | solution.py:162
  347.7 10.4 %collective-permute-start.39 = (f32[8,8192]{1,0:T(8,128)S(1)}, f32[8,8192]{1,0:T(8,128)S(1)}, u32[]{:S(2)}, u32[]{:S(2)}) collective-permute-start(f32[8,8192]{1,0:T(8,128)S(1)} %get-tuple-element.32), channel_id=1, source_target_pairs={{0,224},{8,232},{16,240},{24,248},{32,0},{40,8},{48,16},{56,24},{6... | collective-permute-start | bytes 786440 | tf_op jit(solution)/shard_map/ppermute | solution.py:162
  350.9 10.3 %collective-permute-start.32 = (f32[8,8192]{1,0:T(8,128)S(1)}, f32[8,8192]{1,0:T(8,128)S(1)}, u32[]{:S(2)}, u32[]{:S(2)}) collective-permute-start(f32[8,8192]{1,0:T(8,128)S(1)} %get-tuple-element.33), channel_id=1, source_target_pairs={{0,224},{8,232},{16,240},{24,248},{32,0},{40,8},{48,16},{56,24},{6... | collective-permute-start | bytes 786440 | tf_op jit(solution)/shard_map/ppermute | solution.py:162
  363.7 9.9 %collective-permute-start.40 = (f32[8,8192]{1,0:T(8,128)S(1)}, f32[8,8192]{1,0:T(8,128)S(1)}, u32[]{:S(2)}, u32[]{:S(2)}) collective-permute-start(f32[8,8192]{1,0:T(8,128)S(1)} %get-tuple-element.28), channel_id=1, source_target_pairs={{0,224},{8,232},{16,240},{24,248},{32,0},{40,8},{48,16},{56,24},{6... | collective-permute-start | bytes 786440 | tf_op jit(solution)/shard_map/ppermute | solution.py:162
  378.8 10.3 %collective-permute-start.20 = (f32[8,8192]{1,0:T(8,128)S(1)}, f32[8,8192]{1,0:T(8,128)S(1)}, u32[]{:S(2)}, u32[]{:S(2)}) collective-permute-start(f32[8,8192]{1,0:T(8,128)S(1)} %get-tuple-element.23), channel_id=1, source_target_pairs={{0,32},{8,40},{16,48},{24,56},{32,64},{40,72},{48,80},{56,88},{64,... | collective-permute-start | bytes 786440 | tf_op jit(solution)/shard_map/ppermute | solution.py:162
  379.2 10.0 %collective-permute-start.41 = (f32[8,8192]{1,0:T(8,128)S(1)}, f32[8,8192]{1,0:T(8,128)S(1)}, u32[]{:S(2)}, u32[]{:S(2)}) collective-permute-start(f32[8,8192]{1,0:T(8,128)S(1)} %get-tuple-element.24), channel_id=1, source_target_pairs={{0,224},{8,232},{16,240},{24,248},{32,0},{40,8},{48,16},{56,24},{6... | collective-permute-start | bytes 786440 | tf_op jit(solution)/shard_map/ppermute | solution.py:162
  394.1 10.2 %collective-permute-start.21 = (f32[8,8192]{1,0:T(8,128)S(1)}, f32[8,8192]{1,0:T(8,128)S(1)}, u32[]{:S(2)}, u32[]{:S(2)}) collective-permute-start(f32[8,8192]{1,0:T(8,128)S(1)} %get-tuple-element.19), channel_id=1, source_target_pairs={{0,32},{8,40},{16,48},{24,56},{32,64},{40,72},{48,80},{56,88},{64,... | collective-permute-start | bytes 786440 | tf_op jit(solution)/shard_map/ppermute | solution.py:162
  394.2 10.1 %collective-permute-start.42 = (f32[8,8192]{1,0:T(8,128)S(1)}, f32[8,8192]{1,0:T(8,128)S(1)}, u32[]{:S(2)}, u32[]{:S(2)}) collective-permute-start(f32[8,8192]{1,0:T(8,128)S(1)} %get-tuple-element.20), channel_id=1, source_target_pairs={{0,224},{8,232},{16,240},{24,248},{32,0},{40,8},{48,16},{56,24},{6... | collective-permute-start | bytes 786440 | tf_op jit(solution)/shard_map/ppermute | solution.py:162
  423.3 10.1 %collective-permute-start.23 = (f32[8,8192]{1,0:T(8,128)S(1)}, f32[8,8192]{1,0:T(8,128)S(1)}, u32[]{:S(2)}, u32[]{:S(2)}) collective-permute-start(f32[8,8192]{1,0:T(8,128)S(1)} %get-tuple-element.11), channel_id=1, source_target_pairs={{0,32},{8,40},{16,48},{24,56},{32,64},{40,72},{48,80},{56,88},{64,... | collective-permute-start | bytes 786440 | tf_op jit(solution)/shard_map/ppermute | solution.py:162
  423.4 10.0 %collective-permute-start.44 = (f32[8,8192]{1,0:T(8,128)S(1)}, f32[8,8192]{1,0:T(8,128)S(1)}, u32[]{:S(2)}, u32[]{:S(2)}) collective-permute-start(f32[8,8192]{1,0:T(8,128)S(1)} %get-tuple-element.12), channel_id=1, source_target_pairs={{0,224},{8,232},{16,240},{24,248},{32,0},{40,8},{48,16},{56,24},{6... | collective-permute-start | bytes 786440 | tf_op jit(solution)/shard_map/ppermute | solution.py:162
  437.9 10.8 %collective-permute-start.45 = (f32[16,8192]{1,0:T(8,128)S(1)}, f32[16,8192]{1,0:T(8,128)S(1)}, u32[]{:S(2)}, u32[]{:S(2)}) collective-permute-start(f32[16,8192]{1,0:T(8,128)S(1)} %fusion.37), channel_id=1, source_target_pairs={{0,16},{8,24},{16,0},{24,8},{32,48},{40,56},{48,32},{56,40},{64,80... | collective-permute-start | bytes 1572872 | tf_op jit(solution)/shard_map/ppermute | solution.py:169
  (33 other events, 295.5 us)
